TPU v7x, 32 devices: a whole 2x2x4 slice. The times are simulated.
32 devices in a mesh: case: 2 (over y), tm: 4 (over z), bundle: 2 (over x), sub: 2 (over core).
Axes of the slice: x: 2, y: 2, z: 4, core: 2. Of those that a mesh axis runs over, the one named last changes fastest.
Arguments:
- cotangent: bfloat16 [16384, 512], P(('case', 'tm'), 'bundle'), parts along dimension 0, may hold values from -28 to 28
- inputs: bfloat16 [16384, 512], P(('case', 'tm'), 'bundle'), parts along dimension 0, may hold values from -6 to 6
- impulse: bfloat16 [8, 128, 4096], P('bundle', 'sub'), may hold values from -0.0625 to 0.0625
- terminal: int32 [8, 64], P('bundle'), may hold values from 0 to 63, each once within a row
- fault_step: int32 [2], P('case'), parts along dimension 0, may hold values from 0 to 4095
Outputs:
- voltage_grad: bfloat16 [16384, 512], P(('case', 'tm', 'sub'), 'bundle'), parts along dimension 0
- impulse_grad: float32 [16, 128, 4096], P(('case', 'bundle'), 'sub', 'tm'), parts along dimension 0
There are 2 independent parts, one for each index of `case`. A program takes and returns all parts, laid end to end along the dimension named above; an argument that names none is the same for every part. Nothing has to cross between parts.
Inputs may be any that keep to these rules, and one draw needn't show every extreme that they name: Each row of terminal orders the 64 terminals of a bundle, each once.
All inputs are finite; a program needn't handle non-finite values.
Results may differ from a plain program's by a relative error of at most 0.001.
Values may be sent and summed in bfloat16 or wider, within the bound.
No kernel may reach another device: no remote copies, remote signals or barrier semaphores. Data moves between devices by JAX's collectives and lax.ppermute only.
A program may use at most 320 MiB of HBM per device.

v0:
```python
import functools
import math

import jax
import jax.numpy as jnp
from jax import lax
from jax.experimental import pallas as pl
from jax.experimental.pallas import tpu as pltpu
from jax.sharding import PartitionSpec as P


CB = 64
NB = 8
L = 128


norm_ratio = 0.5
tile_rows = 4
chunk_rows = 256
_INTERPRET = False


def passed_along(block, axis, distance):
    devices = range(lax.axis_size(axis))
    route = [(i - distance, i) for i in devices if i - distance in devices]
    return lax.ppermute(block, axis, route)


def lags_span(all_lags, band):
    return band * (all_lags // band + 1) + 1


def dx_kernel(r_ref, t_ref, o_ref, *, lag_tiles, rows):
    width = o_ref.shape[2]
    width_t = t_ref.shape[2]
    for c in range(rows // chunk_rows):
        base = c * chunk_rows
        acc = jnp.zeros((chunk_rows, width), jnp.float32)
        for q in range(lag_tiles):
            x = r_ref[0, base + q : base + q + chunk_rows, :].astype(jnp.bfloat16)
            acc = acc + jnp.dot(x, t_ref[0, q * width_t : (q + 1) * width_t, :], preferred_element_type=jnp.float32)
        o_ref[0, base : base + chunk_rows, :] = acc


def raw_kernel(rt_ref, m_ref, o_ref, acc_ref, *, lag_steps, rows, chunk, pad, lags):
    band = 16
    acc_ref[...] = jnp.zeros(acc_ref.shape, jnp.float32)
    rt = rt_ref[0]
    top = lag_steps - 1
    for q in range(lag_steps):
        m = m_ref[0, top - q : top - q + rows, :].astype(jnp.bfloat16)
        g = jnp.dot(rt, m, preferred_element_type=jnp.float32)
        for v in range(band // 2):
            first = (band * q - 2 * v + pad) * chunk
            acc_ref[first : first + band * chunk, :] += g[:, v * 2 * CB : (v + 1) * 2 * CB]
    lo = acc_ref[pad * chunk : (pad + lags) * chunk, :]
    hi = acc_ref[(pad + 1) * chunk : (pad + 1 + lags) * chunk, :]
    o_ref[0] = lo[:, :CB] + hi[:, CB:]


def local_body(cotangent, inputs, impulse, terminal, fault_step):
    seg_rows = cotangent.shape[0]
    nb = terminal.shape[0]
    width = terminal.shape[1]
    lag_count = impulse.shape[1]
    n_sub = lax.axis_size("sub")
    sub = lax.axis_index("sub")
    all_lags = lag_count * n_sub
    tr = tile_rows
    rows4 = seg_rows // tr
    wide = tr * width
    shift = lag_count // tr
    halo = all_lags // tr
    lag_tiles = shift + 1

    columns = jnp.arange(width, dtype=jnp.int32)
    onehot = (terminal[:, :, None] == columns[None, None, :]).astype(jnp.bfloat16)
    cot4 = cotangent.reshape(rows4, tr, nb, width)
    reord4 = jnp.einsum(
        "ksbi,bir->bksr", cot4, onehot, preferred_element_type=jnp.float32
    ).astype(jnp.bfloat16)
    r4 = reord4.reshape(nb, rows4, wide)

    seg_start = lax.axis_index("tm") * seg_rows
    steps4 = seg_start + tr * jnp.arange(rows4, dtype=jnp.int32)[:, None] + jnp.arange(tr, dtype=jnp.int32)[None, :]
    live4 = steps4 >= fault_step[0]
    inp4 = jnp.transpose(inputs.reshape(rows4, tr, nb, width), (2, 0, 1, 3))
    m4 = jnp.where(live4[None, :, :, None], inp4, jnp.zeros((), jnp.bfloat16)).reshape(nb, rows4, wide)

    ahead = passed_along(r4[:, :halo], "tm", -1)
    r4ext = jnp.concatenate([r4, ahead], axis=1).astype(jnp.float32)
    r4w = lax.dynamic_slice_in_dim(r4ext, sub * shift, rows4 + shift, 1)
    kern = impulse.reshape(nb, lag_count, width, width)
    kpad = jnp.pad(kern, ((0, 0), (tr - 1, tr), (0, 0), (0, 0)))
    stripes = tr * lag_tiles
    toeplitz = jnp.concatenate(
        [lax.slice_in_dim(kpad, tr - 1 - u, tr - 1 - u + stripes, 1, 1) for u in range(tr)], axis=3
    ).reshape(nb, stripes * width, wide)

    partial_dx = pl.pallas_call(
        functools.partial(dx_kernel, lag_tiles=lag_tiles, rows=rows4),
        grid=(nb,),
        in_specs=[
            pl.BlockSpec((1, rows4 + shift, wide), lambda b: (b, 0, 0)),
            pl.BlockSpec((1, tr * lag_tiles * width, wide), lambda b: (b, 0, 0)),
        ],
        out_specs=pl.BlockSpec((1, rows4, wide), lambda b: (b, 0, 0)),
        out_shape=jax.ShapeDtypeStruct((nb, rows4, wide), jnp.float32),
        interpret=_INTERPRET,
    )(r4w, toeplitz)

    n_tm = lax.axis_size("tm")
    half = nb // n_sub
    chunk = width // n_tm
    band = 16
    rows16 = seg_rows * n_tm // band
    lag_steps = all_lags // band + 1
    pad = band
    seg16 = seg_rows // band
    mine = lax.dynamic_slice_in_dim(m4.reshape(nb, seg_rows, width), sub * half, half, 0)
    m_send = mine.reshape(half, seg16, band * width)
    tm_idx = lax.axis_index("tm")
    m_pieces = []
    for e in range(-(n_tm - 1), n_tm):
        if e == 0:
            m_pieces.append(m_send)
            continue
        m_pieces.append(passed_along(m_send, "tm", -e))
    m_relative = jnp.concatenate(m_pieces, axis=1)
    m16 = lax.dynamic_slice_in_dim(m_relative, (n_tm - 1 - tm_idx) * seg16, n_tm * seg16, 1)
    m16 = jnp.pad(m16, ((0, 0), (lag_steps - 1, 0), (0, 0))).astype(jnp.float32)
    reord_mine = lax.dynamic_slice_in_dim(r4.reshape(nb, seg_rows, width), sub * half, half, 0)
    r_split = jnp.transpose(
        reord_mine.reshape(half, seg16, band, n_tm, chunk), (3, 0, 2, 4, 1)
    ).reshape(n_tm, half, band * chunk, seg16)
    own_piece = lax.dynamic_index_in_dim(r_split, tm_idx, 0, keepdims=False)
    pieces = []
    for e in range(-(n_tm - 1), n_tm):
        if e == 0:
            pieces.append(own_piece)
            continue
        wanted = lax.dynamic_index_in_dim(r_split, jnp.clip(tm_idx - e, 0, n_tm - 1), 0, keepdims=False)
        pieces.append(passed_along(wanted, "tm", -e))
    relative = jnp.concatenate(pieces, axis=2)
    r16t = lax.dynamic_slice_in_dim(relative, (n_tm - 1 - tm_idx) * seg16, n_tm * seg16, 2)
    acc_rows = (pad + lags_span(all_lags, band) + pad) * chunk
    raw_half = pl.pallas_call(
        functools.partial(raw_kernel, lag_steps=lag_steps, rows=rows16, chunk=chunk, pad=pad, lags=all_lags),
        grid=(half,),
        in_specs=[
            pl.BlockSpec((1, band * chunk, rows16), lambda b: (b, 0, 0)),
            pl.BlockSpec((1, rows16 + lag_steps - 1, band * width), lambda b: (b, 0, 0)),
        ],
        out_specs=pl.BlockSpec((1, all_lags * chunk, width), lambda b: (b, 0, 0)),
        out_shape=jax.ShapeDtypeStruct((half, all_lags * chunk, width), jnp.float32),
        scratch_shapes=[pltpu.VMEM((acc_rows, 2 * width), jnp.float32)],
        interpret=_INTERPRET,
    )(r16t, m16)
    raw_half = raw_half.reshape(half, all_lags, chunk * width)
    own_raw = lax.all_to_all(raw_half, "sub", 1, 0, tiled=True)

    summed_dx = lax.psum_scatter(partial_dx, "sub", scatter_dimension=1, tiled=True)
    share4 = summed_dx.shape[1]
    own_steps = (
        seg_start
        + sub * share4 * tr
        + tr * jnp.arange(share4, dtype=jnp.int32)[:, None]
        + jnp.arange(tr, dtype=jnp.int32)[None, :]
    )
    dx = jnp.where(
        (own_steps >= fault_step[0])[None, :, :, None],
        summed_dx.reshape(nb, share4, tr, width),
        0.0,
    ).astype(jnp.bfloat16)
    voltage_grad = jnp.transpose(dx, (1, 2, 0, 3)).reshape(share4 * tr, nb * width)

    own_grad = own_raw
    own_squares = jnp.sum(own_grad * own_grad)
    total_squares = own_squares
    for axis in ("sub", "bundle", "tm"):
        total_squares = lax.psum(total_squares, axis)
    norm_limit = norm_ratio * math.sqrt(NB * L * CB * CB)
    factor = norm_limit / jnp.sqrt(total_squares + 1e-06)
    return (voltage_grad, own_grad * factor)


def solution(mesh):
    placed = (
        P(("case", "tm"), "bundle"),
        P(("case", "tm"), "bundle"),
        P("bundle", "sub", None),
        P("bundle", None),
        P("case"),
    )
    return jax.shard_map(
        local_body,
        mesh=mesh,
        in_specs=placed,
        out_specs=(P(("case", "tm", "sub"), "bundle"), P(("case", "bundle"), "sub", "tm")),
        check_vma=False,
    )
```

profile of v0, /device:TPU:0, one launch (start us, length us, event | category | flops | bytes accessed | tf_op | source)
XLA Modules:
  0.0 224.2 jit_solution(14183742652109631251)
XLA Ops:
  7.2 3.3 %reshape.103 = bf16[512,4,4,64]{3,2,1,0:T(4,128)(2,1)S(1)} reshape(bf16[2048,256]{1,0:T(8,128)(2,1)} %param.5) | data formatting | bytes 2097152 | tf_op jit(solution)/shard_map/reshape | solution.py:78
  14.4 6.9 %reshape.105 = bf16[4,64,64,64]{3,2,1,0:T(8,128)(2,1)} reshape(bf16[4,64,4096]{2,1,0:T(8,128)(2,1)} %param.7) | data formatting | bytes 4194304 | tf_op jit(solution)/shard_map/reshape | solution.py:93
  21.2 9.5 %pad_slice_fusion.3 = (bf16[4,68,64,64]{3,2,1,0:T(8,128)(2,1)S(1)}, bf16[4,68,64,64]{3,2,1,0:T(8,128)(2,1)S(1)}, bf16[4,68,64,64]{3,2,1,0:T(8,128)(2,1)S(1)}, bf16[4,68,64,64]{3,2,1,0:T(8,128)(2,1)S(1)}) fusion(bf16[4,64,64,64]{3,2,1,0:T(8,128)(2,1)} %reshape.105), kind=kLoop, calls=%fused_computation.4 | loop fusion | bytes 11010048 | tf_op jit(solution)/shard_map/slice | solution.py:97
  30.8 8.2 %pad_maximum_fusion = bf16[4,68,64,256]{3,2,1,0:T(8,128)(2,1)} fusion(bf16[4,68,64,64]{3,2,1,0:T(8,128)(2,1)S(1)} %get-tuple-element.5, bf16[4,68,64,64]{3,2,1,0:T(8,128)(2,1)S(1)} %get-tuple-element.4, bf16[4,68,64,64]{3,2,1,0:T(8,128)(2,1)S(1)} %get-tuple-element.3, bf16[4,68,64,64]{3,2,1,0:T(8,128)(2,1)S(1)} %get-tuple-element.2), kind=kLoop, calls=%fused_computation | loop fusion | flops 35651584 | bytes 17825792 | tf_op jit(solution)/shard_map/concatenate | solution.py:96
  40.4 3.0 %fusion.6.r_ref = f32[4,528,256]{2,1,0:T(8,128)} fusion(s32[]{:T(128)S(6)} %select_n.32, bf16[4,512,256]{2,1,0:T(8,128)(2,1)} %copy-done, bf16[4,32,256]{2,1,0:T(8,128)(2,1)S(1)} %collective-permute-done), kind=kLoop, calls=%fused_computation.13 | loop fusion | flops 2162688 | bytes 3276804 | tf_op jit(solution)/shard_map/convert_element_type | solution.py:91
  43.4 8.8 %shard_map.68 = f32[4,512,256]{2,1,0:T(8,128)} custom-call(f32[4,528,256]{2,1,0:T(8,128)} %fusion.6.r_ref, bf16[4,4352,256]{2,1,0:T(8,128)(2,1)} %bitcast.43), custom_call_target="tpu_custom_call" | custom-call | tf_op jit(solution)/shard_map/pallas_call | solution.py:100
  52.6 4.5 %reshape.109 = bf16[2,128,16,4,16]{2,1,4,3,0:T(8,128)(2,1)} reshape(bf16[2,2048,64]{1,2,0:T(8,128)(2,1)S(1)} %copy.37) | data formatting | bytes 1048576 | tf_op jit(solution)/shard_map/reshape | solution.py:134
  57.2 3.6 %copy.38 = bf16[4,2,16,16,128]{4,3,2,1,0:T(8,128)(2,1)S(1)} copy(bf16[4,2,16,16,128]{2,4,3,0,1:T(8,128)(2,1)} %bitcast.44) | data formatting | bytes 1048576 | tf_op jit(solution)/shard_map/transpose | solution.py:133
  61.5 7.5 %collective-permute-start.2 = (bf16[2,256,128]{2,1,0:T(8,128)(2,1)S(1)}, bf16[2,256,128]{2,1,0:T(8,128)(2,1)S(1)}, u32[]{:S(2)}, u32[]{:S(2)}) collective-permute-start(bf16[2,256,128]{2,1,0:T(8,128)(2,1)S(1)} %get-tuple-element.10), channel_id=1, source_target_pairs={{0,8},{4,12},{1,9},{5,13},{2,10},{6,14},{3,11},{7,15},{16,24},{20,... | collective-permute-start | bytes 393224 | tf_op jit(solution)/shard_map/ppermute | solution.py:26
  72.2 3.3 %reshape.111 = bf16[512,4,4,64]{3,2,1,0:T(4,128)(2,1)S(1)} reshape(bf16[2048,256]{1,0:T(8,128)(2,1)} %param.6) | data formatting | bytes 2097152 | tf_op jit(solution)/shard_map/reshape | solution.py:87
  75.7 7.0 %broadcast_select_fusion = bf16[512,4,4,64]{3,2,1,0:T(4,128)(2,1)S(1)} fusion(bf16[512,4,4,64]{3,2,1,0:T(4,128)(2,1)S(1)} %reshape.111, pred[512,4]{1,0:T(8,128)(4,1)S(1)} %add_compare_fusion), kind=kLoop, calls=%fused_computation.8 | loop fusion | flops 524288 | bytes 2099200 | tf_op jit(solution)/shard_map/jit(_where)/select_n | solution.py:88
  87.3 6.4 %collective-permute-start.7 = (bf16[2,128,1024]{2,1,0:T(8,128)(2,1)S(1)}, bf16[2,128,1024]{2,1,0:T(8,128)(2,1)S(1)}, u32[]{:S(2)}, u32[]{:S(2)}) collective-permute-start(bf16[2,128,1024]{2,1,0:T(8,128)(2,1)S(1)} %reshape.112), channel_id=1, source_target_pairs={{0,12},{1,13},{2,14},{3,15},{16,28},{17,29},{18,30},{19,31}} | collective-permute-start | bytes 1572872 | tf_op jit(solution)/shard_map/ppermute | solution.py:26
  97.0 14.9 %collective-permute-done.3 = bf16[2,256,128]{2,1,0:T(8,128)(2,1)S(1)} collective-permute-done((bf16[2,256,128]{2,1,0:T(8,128)(2,1)S(1)}, bf16[2,256,128]{2,1,0:T(8,128)(2,1)S(1)}, u32[]{:S(2)}, u32[]{:S(2)}) %collective-permute-start.3) | collective-permute-done | bytes 131104 | tf_op jit(solution)/shard_map/ppermute | solution.py:26
  113.2 16.8 %collective-permute-done.4 = bf16[2,256,128]{2,1,0:T(8,128)(2,1)S(1)} collective-permute-done((bf16[2,256,128]{2,1,0:T(8,128)(2,1)S(1)}, bf16[2,256,128]{2,1,0:T(8,128)(2,1)S(1)}, u32[]{:S(2)}, u32[]{:S(2)}) %collective-permute-start.4) | collective-permute-done | bytes 131104 | tf_op jit(solution)/shard_map/ppermute | solution.py:26
  131.4 3.8 %collective-permute-start.9 = (bf16[2,128,1024]{2,1,0:T(8,128)(2,1)S(1)}, bf16[2,128,1024]{2,1,0:T(8,128)(2,1)S(1)}, u32[]{:S(2)}, u32[]{:S(2)}) collective-permute-start(bf16[2,128,1024]{2,1,0:T(8,128)(2,1)S(1)} %reshape.112), channel_id=1, source_target_pairs={{0,4},{4,8},{8,12},{1,5},{5,9},{9,13},{2,6},{6,10},{10,14},{3,7},{... | collective-permute-start | bytes 1572872 | tf_op jit(solution)/shard_map/ppermute | solution.py:26
  135.3 3.5 %collective-permute-done.6 = bf16[2,256,128]{2,1,0:T(8,128)(2,1)S(1)} collective-permute-done((bf16[2,256,128]{2,1,0:T(8,128)(2,1)S(1)}, bf16[2,256,128]{2,1,0:T(8,128)(2,1)S(1)}, u32[]{:S(2)}, u32[]{:S(2)}) %collective-permute-start.6) | collective-permute-done | bytes 131104 | tf_op jit(solution)/shard_map/ppermute | solution.py:26
  142.3 3.7 %collective-permute-done.9 = bf16[2,128,1024]{2,1,0:T(8,128)(2,1)S(1)} collective-permute-done((bf16[2,128,1024]{2,1,0:T(8,128)(2,1)S(1)}, bf16[2,128,1024]{2,1,0:T(8,128)(2,1)S(1)}, u32[]{:S(2)}, u32[]{:S(2)}) %collective-permute-start.9) | collective-permute-done | bytes 524320 | tf_op jit(solution)/shard_map/ppermute | solution.py:26
  146.1 8.1 %collective-permute-done.10 = bf16[2,128,1024]{2,1,0:T(8,128)(2,1)S(1)} collective-permute-done((bf16[2,128,1024]{2,1,0:T(8,128)(2,1)S(1)}, bf16[2,128,1024]{2,1,0:T(8,128)(2,1)S(1)}, u32[]{:S(2)}, u32[]{:S(2)}) %collective-permute-start.10) | collective-permute-done | bytes 524320 | tf_op jit(solution)/shard_map/ppermute | solution.py:26
  154.2 19.6 %collective-permute-done.11 = bf16[2,128,1024]{2,1,0:T(8,128)(2,1)S(1)} collective-permute-done((bf16[2,128,1024]{2,1,0:T(8,128)(2,1)S(1)}, bf16[2,128,1024]{2,1,0:T(8,128)(2,1)S(1)}, u32[]{:S(2)}, u32[]{:S(2)}) %collective-permute-start.11) | collective-permute-done | bytes 524320 | tf_op jit(solution)/shard_map/ppermute | solution.py:26
  176.5 8.2 %shard_map.69 = f32[2,2048,64]{2,1,0:T(8,128)} custom-call(bf16[2,256,512]{2,1,0:T(8,128)(2,1)} %constant_dynamic-slice_fusion.2.rt_ref, f32[2,520,1024]{2,1,0:T(8,128)} %pad_convert_fusion.m_ref), custom_call_target="tpu_custom_call" | custom-call | tf_op jit(solution)/shard_map/pallas_call | solution.py:147
  187.4 4.6 %all_to_all.4 = f32[2,128,1024]{2,0,1:T(2,128)S(1)} all-to-all(f32[2,128,1024]{2,0,1:T(2,128)S(1)} %copy.40), channel_id=1, replica_groups=mesh['case'=2,'tm'=4,'bundle'=2,'sub'=2] {'sub'}, dimensions={1} | all-to-all | bytes 2097152 | tf_op jit(solution)/shard_map/all_to_all | solution.py:160
  193.7 3.1 %psum.21 = f32[]{:T(128)} all-reduce(f32[]{:T(128)} %multiply_reduce_fusion), channel_id=1, replica_groups=mesh['case'=2,'tm'=4,'bundle'=2,'sub'=2] {'sub'}, use_global_device_ids=true, to_apply=%region_2.3 | all-reduce | flops 1 | bytes 8 | tf_op jit(solution)/shard_map/psum | solution.py:181
  196.8 5.5 %psum.22 = f32[]{:T(128)} all-reduce(f32[]{:T(128)} %psum.21), channel_id=1, replica_groups=mesh['case'=2,'tm'=4,'bundle'=2,'sub'=2] {'bundle'}, use_global_device_ids=true, to_apply=%region_3.4 | all-reduce | flops 1 | bytes 8 | tf_op jit(solution)/shard_map/psum | solution.py:181
  202.3 9.0 %psum.23 = f32[]{:T(128)} all-reduce(f32[]{:T(128)} %psum.22), channel_id=1, replica_groups=mesh['case'=2,'tm'=4,'bundle'=2,'sub'=2] {'tm'}, use_global_device_ids=true, to_apply=%region_4.5 | all-reduce | flops 1 | bytes 8 | tf_op jit(solution)/shard_map/psum | solution.py:181
  (62 shorter events, 35.7 us)
Async XLA Ops:
  7.2 206.2 %reduce-scatter.2.cloned.1.call-start = ((), (), s32[]{:S(2)}) async-start(), calls=%async_computation.2 | async-start | bytes 3145728 | tf_op jit(solution)/shard_map/reduce_scatter | solution.py:162
  13.0 17.7 %copy-start = (bf16[4,512,256]{2,1,0:T(8,128)(2,1)}, bf16[4,512,256]{2,1,0:T(8,128)(2,1)S(1)}, u32[]{:S(2)}) copy-start(bf16[4,512,256]{2,1,0:T(8,128)(2,1)S(1)} %copy.33) | copy-start | bytes 3145732
  13.1 27.4 %collective-permute-start = (bf16[4,32,256]{2,1,0:T(8,128)(2,1)S(1)}, bf16[4,32,256]{2,1,0:T(8,128)(2,1)S(1)}, u32[]{:S(2)}, u32[]{:S(2)}) collective-permute-start(bf16[4,32,256]{2,1,0:T(8,128)(2,1)S(1)} %slice.20), channel_id=1, source_target_pairs={{4,0},{8,4},{12,8},{5,1},{9,5},{13,9},{6,2},{10,6},{14,10},{7,3},{... | collective-permute-start | bytes 196616 | tf_op jit(solution)/shard_map/ppermute | solution.py:26
  61.5 34.1 %collective-permute-start.2 = (bf16[2,256,128]{2,1,0:T(8,128)(2,1)S(1)}, bf16[2,256,128]{2,1,0:T(8,128)(2,1)S(1)}, u32[]{:S(2)}, u32[]{:S(2)}) collective-permute-start(bf16[2,256,128]{2,1,0:T(8,128)(2,1)S(1)} %get-tuple-element.10), channel_id=1, source_target_pairs={{0,8},{4,12},{1,9},{5,13},{2,10},{6,14},{3,11},{7,15},{16,24},{20,... | collective-permute-start | bytes 393224 | tf_op jit(solution)/shard_map/ppermute | solution.py:26
  69.0 24.7 %collective-permute-start.1 = (bf16[2,256,128]{2,1,0:T(8,128)(2,1)}, bf16[2,256,128]{2,1,0:T(8,128)(2,1)S(1)}, u32[]{:S(2)}, u32[]{:S(2)}) collective-permute-start(bf16[2,256,128]{2,1,0:T(8,128)(2,1)} %get-tuple-element.11), channel_id=1, source_target_pairs={{0,12},{1,13},{2,14},{3,15},{16,28},{17,29},{18,30},{19,31}} | collective-permute-start | bytes 393224 | tf_op jit(solution)/shard_map/ppermute | solution.py:26
  84.7 89.1 %collective-permute-start.12 = (bf16[2,128,1024]{2,1,0:T(8,128)(2,1)S(1)}, bf16[2,128,1024]{2,1,0:T(8,128)(2,1)S(1)}, u32[]{:S(2)}, u32[]{:S(2)}) collective-permute-start(bf16[2,128,1024]{2,1,0:T(8,128)(2,1)S(1)} %reshape.112), channel_id=1, source_target_pairs={{12,0},{13,1},{14,2},{15,3},{28,16},{29,17},{30,18},{31,19}} | collective-permute-start | bytes 1572872 | tf_op jit(solution)/shard_map/ppermute | solution.py:26
  86.0 56.3 %collective-permute-start.8 = (bf16[2,128,1024]{2,1,0:T(8,128)(2,1)S(1)}, bf16[2,128,1024]{2,1,0:T(8,128)(2,1)S(1)}, u32[]{:S(2)}, u32[]{:S(2)}) collective-permute-start(bf16[2,128,1024]{2,1,0:T(8,128)(2,1)S(1)} %reshape.112), channel_id=1, source_target_pairs={{0,8},{4,12},{1,9},{5,13},{2,10},{6,14},{3,11},{7,15},{16,24},{20,... | collective-permute-start | bytes 1572872 | tf_op jit(solution)/shard_map/ppermute | solution.py:26
  87.3 53.6 %collective-permute-start.7 = (bf16[2,128,1024]{2,1,0:T(8,128)(2,1)S(1)}, bf16[2,128,1024]{2,1,0:T(8,128)(2,1)S(1)}, u32[]{:S(2)}, u32[]{:S(2)}) collective-permute-start(bf16[2,128,1024]{2,1,0:T(8,128)(2,1)S(1)} %reshape.112), channel_id=1, source_target_pairs={{0,12},{1,13},{2,14},{3,15},{16,28},{17,29},{18,30},{19,31}} | collective-permute-start | bytes 1572872 | tf_op jit(solution)/shard_map/ppermute | solution.py:26
  93.7 18.2 %collective-permute-start.3 = (bf16[2,256,128]{2,1,0:T(8,128)(2,1)S(1)}, bf16[2,256,128]{2,1,0:T(8,128)(2,1)S(1)}, u32[]{:S(2)}, u32[]{:S(2)}) collective-permute-start(bf16[2,256,128]{2,1,0:T(8,128)(2,1)S(1)} %get-tuple-element.9), channel_id=1, source_target_pairs={{0,4},{4,8},{8,12},{1,5},{5,9},{9,13},{2,6},{6,10},{10,14},{3,7},{... | collective-permute-start | bytes 393224 | tf_op jit(solution)/shard_map/ppermute | solution.py:26
  95.6 35.8 %collective-permute-start.5 = (bf16[2,256,128]{2,1,0:T(8,128)(2,1)S(1)}, bf16[2,256,128]{2,1,0:T(8,128)(2,1)S(1)}, u32[]{:S(2)}, u32[]{:S(2)}) collective-permute-start(bf16[2,256,128]{2,1,0:T(8,128)(2,1)S(1)} %get-tuple-element.7), channel_id=1, source_target_pairs={{8,0},{12,4},{9,1},{13,5},{10,2},{14,6},{11,3},{15,7},{24,16},{28,... | collective-permute-start | bytes 393224 | tf_op jit(solution)/shard_map/ppermute | solution.py:26
  111.9 18.2 %collective-permute-start.4 = (bf16[2,256,128]{2,1,0:T(8,128)(2,1)S(1)}, bf16[2,256,128]{2,1,0:T(8,128)(2,1)S(1)}, u32[]{:S(2)}, u32[]{:S(2)}) collective-permute-start(bf16[2,256,128]{2,1,0:T(8,128)(2,1)S(1)} %get-tuple-element.8), channel_id=1, source_target_pairs={{4,0},{8,4},{12,8},{5,1},{9,5},{13,9},{6,2},{10,6},{14,10},{7,3},{... | collective-permute-start | bytes 393224 | tf_op jit(solution)/shard_map/ppermute | solution.py:26
  130.1 8.6 %collective-permute-start.6 = (bf16[2,256,128]{2,1,0:T(8,128)(2,1)S(1)}, bf16[2,256,128]{2,1,0:T(8,128)(2,1)S(1)}, u32[]{:S(2)}, u32[]{:S(2)}) collective-permute-start(bf16[2,256,128]{2,1,0:T(8,128)(2,1)S(1)} %get-tuple-element.6), channel_id=1, source_target_pairs={{12,0},{13,1},{14,2},{15,3},{28,16},{29,17},{30,18},{31,19}} | collective-permute-start | bytes 393224 | tf_op jit(solution)/shard_map/ppermute | solution.py:26
  131.4 14.5 %collective-permute-start.9 = (bf16[2,128,1024]{2,1,0:T(8,128)(2,1)S(1)}, bf16[2,128,1024]{2,1,0:T(8,128)(2,1)S(1)}, u32[]{:S(2)}, u32[]{:S(2)}) collective-permute-start(bf16[2,128,1024]{2,1,0:T(8,128)(2,1)S(1)} %reshape.112), channel_id=1, source_target_pairs={{0,4},{4,8},{8,12},{1,5},{5,9},{9,13},{2,6},{6,10},{10,14},{3,7},{... | collective-permute-start | bytes 1572872 | tf_op jit(solution)/shard_map/ppermute | solution.py:26
  138.7 15.4 %collective-permute-start.10 = (bf16[2,128,1024]{2,1,0:T(8,128)(2,1)S(1)}, bf16[2,128,1024]{2,1,0:T(8,128)(2,1)S(1)}, u32[]{:S(2)}, u32[]{:S(2)}) collective-permute-start(bf16[2,128,1024]{2,1,0:T(8,128)(2,1)S(1)} %reshape.112), channel_id=1, source_target_pairs={{4,0},{8,4},{12,8},{5,1},{9,5},{13,9},{6,2},{10,6},{14,10},{7,3},{... | collective-permute-start | bytes 1572872 | tf_op jit(solution)/shard_map/ppermute | solution.py:26
  140.9 32.8 %collective-permute-start.11 = (bf16[2,128,1024]{2,1,0:T(8,128)(2,1)S(1)}, bf16[2,128,1024]{2,1,0:T(8,128)(2,1)S(1)}, u32[]{:S(2)}, u32[]{:S(2)}) collective-permute-start(bf16[2,128,1024]{2,1,0:T(8,128)(2,1)S(1)} %reshape.112), channel_id=1, source_target_pairs={{8,0},{12,4},{9,1},{13,5},{10,2},{14,6},{11,3},{15,7},{24,16},{28,... | collective-permute-start | bytes 1572872 | tf_op jit(solution)/shard_map/ppermute | solution.py:26
Sparse Core Ops, SparseCore 0:
  52.3 13.4 reduce-scatter.1
where the time goes:
time: 225 us; the launch traced here: 224 us
  waiting for transfers between devices  66.6 us (30%)
  local copies, waits for them, and re-layouts  45.7 us (20%)
  starting transfers between devices  32.4 us (14%)
  other arithmetic  22.7 us (10%)
  blocking collectives  22.2 us (10%)
  Pallas kernels  16.9 us (8%)
  between operations  15.8 us (7%)
    ppermute x13, waiting for transfers between devices, passed_along(): return lax.ppermute(block, axis, route)  66.6 us
    ppermute x13, starting transfers between devices, passed_along(): return lax.ppermute(block, axis, route)  32.4 us
    psum x3, blocking collectives, local_body(): total_squares = lax.psum(total_squares, axis)  17.6 us
    slice x1, local copies, waits for them, and re-layouts, local_body(): lax.slice_in_dim(kpad, tr - 1 - u, tr - 1 - u + stripes, 1, 1)  9.52 us
    pallas_call x1, Pallas kernels, local_body(): pl.pallas_call(functools.partial(dx_kernel, lag_tiles=lag_tiles, rows=row...  8.77 us
    concatenate x1, other arithmetic, local_body(): jnp.concatenate([lax.slice_in_dim(kpad, tr - 1 - u, tr - 1 - u + stripes,...  8.24 us
    pallas_call x1, Pallas kernels, local_body(): pl.pallas_call(functools.partial(raw_kernel, lag_steps=lag_steps, rows=ro...  8.16 us
    select_n x1, other arithmetic, local_body(): jnp.where(live4[None, :, :, None], inp4, jnp.zeros((), jnp.bfloat16))  6.98 us
  transfers between devices with their start and end apart: 14, of which 6 were waited for; matrix products, arithmetic and copies ran while one was open for 26% of the time, Pallas kernels for 4%

commit v1 on v0

--- a/solution.py
+++ b/solution.py
@@ -82,11 +82,6 @@
     r4 = reord4.reshape(nb, rows4, wide)
 
     seg_start = lax.axis_index("tm") * seg_rows
-    steps4 = seg_start + tr * jnp.arange(rows4, dtype=jnp.int32)[:, None] + jnp.arange(tr, dtype=jnp.int32)[None, :]
-    live4 = steps4 >= fault_step[0]
-    inp4 = jnp.transpose(inputs.reshape(rows4, tr, nb, width), (2, 0, 1, 3))
-    m4 = jnp.where(live4[None, :, :, None], inp4, jnp.zeros((), jnp.bfloat16)).reshape(nb, rows4, wide)
-
     ahead = passed_along(r4[:, :halo], "tm", -1)
     r4ext = jnp.concatenate([r4, ahead], axis=1).astype(jnp.float32)
     r4w = lax.dynamic_slice_in_dim(r4ext, sub * shift, rows4 + shift, 1)
@@ -117,8 +112,12 @@
     lag_steps = all_lags // band + 1
     pad = band
     seg16 = seg_rows // band
-    mine = lax.dynamic_slice_in_dim(m4.reshape(nb, seg_rows, width), sub * half, half, 0)
-    m_send = mine.reshape(half, seg16, band * width)
+    inp16 = jnp.transpose(inputs.reshape(seg16, band, nb, width), (2, 0, 1, 3))
+    inp16 = lax.dynamic_slice_in_dim(inp16, sub * half, half, 0)
+    steps16 = seg_start + band * jnp.arange(seg16, dtype=jnp.int32)[:, None] + jnp.arange(band, dtype=jnp.int32)[None, :]
+    m_send = jnp.where(
+        (steps16 >= fault_step[0])[None, :, :, None], inp16, jnp.zeros((), jnp.bfloat16)
+    ).reshape(half, seg16, band * width)
     tm_idx = lax.axis_index("tm")
     m_pieces = []
     for e in range(-(n_tm - 1), n_tm):
@@ -129,10 +128,11 @@
     m_relative = jnp.concatenate(m_pieces, axis=1)
     m16 = lax.dynamic_slice_in_dim(m_relative, (n_tm - 1 - tm_idx) * seg16, n_tm * seg16, 1)
     m16 = jnp.pad(m16, ((0, 0), (lag_steps - 1, 0), (0, 0))).astype(jnp.float32)
-    reord_mine = lax.dynamic_slice_in_dim(r4.reshape(nb, seg_rows, width), sub * half, half, 0)
-    r_split = jnp.transpose(
-        reord_mine.reshape(half, seg16, band, n_tm, chunk), (3, 0, 2, 4, 1)
-    ).reshape(n_tm, half, band * chunk, seg16)
+    cot16 = lax.dynamic_slice_in_dim(cotangent.reshape(seg16, band, nb, width), sub * half, half, 2)
+    onehot_mine = lax.dynamic_slice_in_dim(onehot, sub * half, half, 0).reshape(half, width, n_tm, chunk)
+    r_split = jnp.einsum(
+        "ksbi,bicr->cbsrk", cot16, onehot_mine, preferred_element_type=jnp.float32
+    ).astype(jnp.bfloat16).reshape(n_tm, half, band * chunk, seg16)
     own_piece = lax.dynamic_index_in_dim(r_split, tm_idx, 0, keepdims=False)
     pieces = []
     for e in range(-(n_tm - 1), n_tm):
@@ -176,9 +176,7 @@
 
     own_grad = own_raw
     own_squares = jnp.sum(own_grad * own_grad)
-    total_squares = own_squares
-    for axis in ("sub", "bundle", "tm"):
-        total_squares = lax.psum(total_squares, axis)
+    total_squares = lax.psum(lax.psum(own_squares, ("bundle", "sub")), "tm")
     norm_limit = norm_ratio * math.sqrt(NB * L * CB * CB)
     factor = norm_limit / jnp.sqrt(total_squares + 1e-06)
     return (voltage_grad, own_grad * factor)

time: 225 us -> 235 us (1.044)
  waiting for transfers between devices: 66.6 us -> 92.4 us
  starting transfers between devices: 32.4 us -> 25.8 us
  other arithmetic: 22.7 us -> 17.2 us
  local copies, waits for them, and re-layouts: 45.7 us -> 41.7 us
    ppermute x13, waiting for transfers between devices: 66.6 us -> 92.4 us  [passed_along(): return lax.ppermute(block, axis, route)]
    ppermute x13, starting transfers between devices: 32.4 us -> 25.8 us  [passed_along(): return lax.ppermute(block, axis, route)]
    select_n x1, other arithmetic: 6.98 us -> 2.8 us  [local_body(): jnp.where((steps16 >= fault_step[0])[None, :, :, None], inp16, jnp.zeros(...]
    transpose x1 -> x0, local copies, waits for them, and re-layouts: 3.59 us -> none  [local_body(): jnp.transpose(reord_mine.reshape(half, seg16, band, n_tm, chunk), (3, 0,...]
    unnamed x15 -> x19, local copies, waits for them, and re-layouts: 0.56 us -> 3.04 us
    psum x3 -> x2, blocking collectives: 17.6 us -> 16.5 us  [local_body(): total_squares = lax.psum(lax.psum(own_squares, ('bundle', 'sub')), 'tm')]
  transfers between devices with their start and end apart: 14 -> 14, of which waited for: 6 -> 4; matrix products, arithmetic and copies ran while one was open for 26% -> 20% of each run, Pallas kernels for 4% -> 3%
where the time goes in v1:
time: 235 us; the launch traced here: 234 us
  waiting for transfers between devices  92.4 us (39%)
  local copies, waits for them, and re-layouts  41.7 us (18%)
  starting transfers between devices  25.8 us (11%)
  blocking collectives  21 us (9%)
  other arithmetic  17.2 us (7%)
  Pallas kernels  16.9 us (7%)
  between operations  15.9 us (7%)
  matrix products  3.21 us (1%)
    ppermute x13, waiting for transfers between devices, passed_along(): return lax.ppermute(block, axis, route)  92.4 us
    ppermute x13, starting transfers between devices, passed_along(): return lax.ppermute(block, axis, route)  25.8 us
    psum x2, blocking collectives, local_body(): total_squares = lax.psum(lax.psum(own_squares, ('bundle', 'sub')), 'tm')  16.5 us
    slice x1, local copies, waits for them, and re-layouts, local_body(): lax.slice_in_dim(kpad, tr - 1 - u, tr - 1 - u + stripes, 1, 1)  9.32 us
    pallas_call x1, Pallas kernels, local_body(): pl.pallas_call(functools.partial(dx_kernel, lag_tiles=lag_tiles, rows=row...  8.77 us
    concatenate x1, other arithmetic, local_body(): jnp.concatenate([lax.slice_in_dim(kpad, tr - 1 - u, tr - 1 - u + stripes,...  8.25 us
    pallas_call x1, Pallas kernels, local_body(): pl.pallas_call(functools.partial(raw_kernel, lag_steps=lag_steps, rows=ro...  8.15 us
    reshape x1, local copies, waits for them, and re-layouts, local_body(): kern = impulse.reshape(nb, lag_count, width, width)  5.55 us
  transfers between devices with their start and end apart: 14, of which 4 were waited for; matrix products, arithmetic and copies ran while one was open for 20% of the time, Pallas kernels for 3%

profile of v1, /device:TPU:0, one launch (start us, length us, event | category | flops | bytes accessed | tf_op | source)
XLA Modules:
  0.0 234.2 jit_solution(12909044258224534140)
XLA Ops:
  7.2 3.3 %reshape.106 = bf16[512,4,4,64]{3,2,1,0:T(4,128)(2,1)S(1)} reshape(bf16[2048,256]{1,0:T(8,128)(2,1)} %param.5) | data formatting | bytes 2097152 | tf_op jit(solution)/shard_map/reshape | solution.py:78
  10.5 2.9 %fusion.2 = bf16[4,64,512,4]{2,1,3,0:T(8,128)(2,1)} fusion(bf16[512,4,4,64]{3,2,1,0:T(4,128)(2,1)S(1)} %reshape.106, s32[4,64]{1,0:T(4,128)} %param.8), kind=kOutput, calls=%fused_computation.9 | convolution fusion | flops 67649536 | bytes 2098176 | tf_op jit(solution)/shard_map/ksbi,bir->bksr/dot_general | solution.py:79
  16.6 5.5 %reshape.108 = bf16[4,64,64,64]{3,2,1,0:T(8,128)(2,1)} reshape(bf16[4,64,4096]{2,1,0:T(8,128)(2,1)S(1)} %copy-done.1) | data formatting | bytes 4194304 | tf_op jit(solution)/shard_map/reshape | solution.py:88
  22.2 9.3 %pad_slice_fusion.3 = (bf16[4,68,64,64]{3,2,1,0:T(8,128)(2,1)S(1)}, bf16[4,68,64,64]{3,2,1,0:T(8,128)(2,1)S(1)}, bf16[4,68,64,64]{3,2,1,0:T(8,128)(2,1)S(1)}, bf16[4,68,64,64]{3,2,1,0:T(8,128)(2,1)S(1)}) fusion(bf16[4,64,64,64]{3,2,1,0:T(8,128)(2,1)} %reshape.108), kind=kLoop, calls=%fused_computation.4 | loop fusion | bytes 11010048 | tf_op jit(solution)/shard_map/slice | solution.py:92
  31.5 8.3 %pad_maximum_fusion = bf16[4,68,64,256]{3,2,1,0:T(8,128)(2,1)} fusion(bf16[4,68,64,64]{3,2,1,0:T(8,128)(2,1)S(1)} %get-tuple-element.5, bf16[4,68,64,64]{3,2,1,0:T(8,128)(2,1)S(1)} %get-tuple-element.4, bf16[4,68,64,64]{3,2,1,0:T(8,128)(2,1)S(1)} %get-tuple-element.3, bf16[4,68,64,64]{3,2,1,0:T(8,128)(2,1)S(1)} %get-tuple-element.2), kind=kLoop, calls=%fused_computation | loop fusion | flops 35651584 | bytes 17825792 | tf_op jit(solution)/shard_map/concatenate | solution.py:91
  39.8 3.3 %reshape.113 = bf16[128,16,4,64]{3,2,1,0:T(4,128)(2,1)S(1)} reshape(bf16[2048,256]{1,0:T(8,128)(2,1)} %param.5) | data formatting | bytes 2097152 | tf_op jit(solution)/shard_map/reshape | solution.py:131
  43.1 1.8 fusion.6.r_ref
  44.9 8.8 %shard_map.68 = f32[4,512,256]{2,1,0:T(8,128)} custom-call(f32[4,528,256]{2,1,0:T(8,128)} %fusion.6.r_ref, bf16[4,4352,256]{2,1,0:T(8,128)(2,1)} %bitcast.66), custom_call_target="tpu_custom_call" | custom-call | tf_op jit(solution)/shard_map/pallas_call | solution.py:95
  57.7 8.0 %collective-permute-start.1 = (bf16[2,256,128]{2,1,0:T(8,128)(2,1)}, bf16[2,256,128]{2,1,0:T(8,128)(2,1)S(1)}, u32[]{:S(2)}, u32[]{:S(2)}) collective-permute-start(bf16[2,256,128]{2,1,0:T(8,128)(2,1)} %get-tuple-element.11), channel_id=1, source_target_pairs={{0,12},{1,13},{2,14},{3,15},{16,28},{17,29},{18,30},{19,31}} | collective-permute-start | bytes 393224 | tf_op jit(solution)/shard_map/ppermute | solution.py:26
  67.7 3.3 %reshape.115 = bf16[128,16,4,64]{3,2,1,0:T(4,128)(2,1)S(1)} reshape(bf16[2048,256]{1,0:T(8,128)(2,1)} %param.6) | data formatting | bytes 2097152 | tf_op jit(solution)/shard_map/reshape | solution.py:115
  71.1 2.8 %fusion.7 = bf16[2,128,16,64]{3,0,2,1:T(2,128)(2,1)S(1)} fusion(pred[128,16]{1,0:T(8,128)(4,1)S(1)} %add_compare_fusion, bf16[128,16,4,64]{3,2,1,0:T(4,128)(2,1)S(1)} %reshape.115, s32[]{:T(128)S(6)} %select_n.35), kind=kLoop, calls=%fused_computation.15 | loop fusion | flops 262144 | bytes 1050628 | tf_op jit(solution)/shard_map/jit(_where)/select_n | solution.py:118
  77.8 2.5 %collective-permute-start.9 = (bf16[2,128,1024]{2,1,0:T(8,128)(2,1)S(1)}, bf16[2,128,1024]{2,1,0:T(8,128)(2,1)S(1)}, u32[]{:S(2)}, u32[]{:S(2)}) collective-permute-start(bf16[2,128,1024]{2,1,0:T(8,128)(2,1)S(1)} %copy.55), channel_id=1, source_target_pairs={{0,4},{4,8},{8,12},{1,5},{5,9},{9,13},{2,6},{6,10},{10,14},{3,7},{... | collective-permute-start | bytes 1572872 | tf_op jit(solution)/shard_map/ppermute | solution.py:26
  80.3 1.9 collective-permute-start.3
  83.6 29.3 %collective-permute-done.3 = bf16[2,256,128]{2,1,0:T(8,128)(2,1)S(1)} collective-permute-done((bf16[2,256,128]{2,1,0:T(8,128)(2,1)}, bf16[2,256,128]{2,1,0:T(8,128)(2,1)S(1)}, u32[]{:S(2)}, u32[]{:S(2)}) %collective-permute-start.3) | collective-permute-done | bytes 131104 | tf_op jit(solution)/shard_map/ppermute | solution.py:26
  116.7 21.4 %collective-permute-done.5 = bf16[2,256,128]{2,1,0:T(8,128)(2,1)S(1)} collective-permute-done((bf16[2,256,128]{2,1,0:T(8,128)(2,1)}, bf16[2,256,128]{2,1,0:T(8,128)(2,1)S(1)}, u32[]{:S(2)}, u32[]{:S(2)}) %collective-permute-start.5) | collective-permute-done | bytes 131104 | tf_op jit(solution)/shard_map/ppermute | solution.py:26
  143.1 11.4 %collective-permute-done.10 = bf16[2,128,1024]{2,1,0:T(8,128)(2,1)S(1)} collective-permute-done((bf16[2,128,1024]{2,1,0:T(8,128)(2,1)S(1)}, bf16[2,128,1024]{2,1,0:T(8,128)(2,1)S(1)}, u32[]{:S(2)}, u32[]{:S(2)}) %collective-permute-start.10) | collective-permute-done | bytes 524320 | tf_op jit(solution)/shard_map/ppermute | solution.py:26
  154.6 30.3 %collective-permute-done.11 = bf16[2,128,1024]{2,1,0:T(8,128)(2,1)S(1)} collective-permute-done((bf16[2,128,1024]{2,1,0:T(8,128)(2,1)S(1)}, bf16[2,128,1024]{2,1,0:T(8,128)(2,1)S(1)}, u32[]{:S(2)}, u32[]{:S(2)}) %collective-permute-start.11) | collective-permute-done | bytes 524320 | tf_op jit(solution)/shard_map/ppermute | solution.py:26
  185.2 2.4 %pad_convert_fusion.m_ref = f32[2,520,1024]{2,1,0:T(8,128)} fusion(bf16[2,512,1024]{2,1,0:T(8,128)(2,1)S(1)} %constant_dynamic-slice_fusion), kind=kLoop, calls=%fused_computation.5 | loop fusion | flops 1064960 | bytes 6356992 | tf_op jit(solution)/shard_map/convert_element_type | solution.py:130
  187.6 8.2 %shard_map.69 = f32[2,2048,64]{2,1,0:T(8,128)} custom-call(bf16[2,256,512]{2,1,0:T(8,128)(2,1)} %constant_dynamic-slice_fusion.1.rt_ref, f32[2,520,1024]{2,1,0:T(8,128)} %pad_convert_fusion.m_ref), custom_call_target="tpu_custom_call" | custom-call | tf_op jit(solution)/shard_map/pallas_call | solution.py:147
  195.8 2.0 reshape.117
  198.6 4.6 %all_to_all.4 = f32[2,128,1024]{2,0,1:T(2,128)S(1)} all-to-all(f32[2,128,1024]{2,0,1:T(2,128)S(1)} %copy.62), channel_id=1, replica_groups=mesh['case'=2,'tm'=4,'bundle'=2,'sub'=2] {'sub'}, dimensions={1} | all-to-all | bytes 2097152 | tf_op jit(solution)/shard_map/all_to_all | solution.py:160
  203.2 1.7 multiply_reduce_fusion
  204.9 7.5 %psum.14 = f32[]{:T(128)} all-reduce(f32[]{:T(128)} %multiply_reduce_fusion), channel_id=1, replica_groups=mesh['case'=2,'tm'=4,'bundle'=2,'sub'=2] {'bundle','sub'}, use_global_device_ids=true, to_apply=%region_2.3 | all-reduce | flops 1 | bytes 8 | tf_op jit(solution)/shard_map/psum | solution.py:179
  212.4 9.0 %psum.15 = f32[]{:T(128)} all-reduce(f32[]{:T(128)} %psum.14), channel_id=1, replica_groups=mesh['case'=2,'tm'=4,'bundle'=2,'sub'=2] {'tm'}, use_global_device_ids=true, to_apply=%region_3.4 | all-reduce | flops 1 | bytes 8 | tf_op jit(solution)/shard_map/psum | solution.py:179
  (65 shorter events, 28.9 us)
Async XLA Ops:
  7.2 216.2 %reduce-scatter.2.cloned.1.call-start = ((), (), s32[]{:S(2)}) async-start(), calls=%async_computation.2 | async-start | bytes 3145728 | tf_op jit(solution)/shard_map/reduce_scatter | solution.py:162
  13.5 3.1 %copy-start.1 = (bf16[4,64,4096]{2,1,0:T(8,128)(2,1)S(1)}, bf16[4,64,4096]{2,1,0:T(8,128)(2,1)}, u32[]{:S(2)}) copy-start(bf16[4,64,4096]{2,1,0:T(8,128)(2,1)} %param.7) | copy-start | bytes 6291460
  15.1 28.0 %collective-permute-start = (bf16[4,32,256]{2,1,0:T(8,128)(2,1)S(1)}, bf16[4,32,256]{2,1,0:T(8,128)(2,1)S(1)}, u32[]{:S(2)}, u32[]{:S(2)}) collective-permute-start(bf16[4,32,256]{2,1,0:T(8,128)(2,1)S(1)} %slice.20), channel_id=1, source_target_pairs={{4,0},{8,4},{12,8},{5,1},{9,5},{13,9},{6,2},{10,6},{14,10},{7,3},{... | collective-permute-start | bytes 196616 | tf_op jit(solution)/shard_map/ppermute | solution.py:26
  31.5 8.3 %copy-start.2 = (s32[4,64]{1,0:T(4,128)S(1)}, s32[4,64]{1,0:T(4,128)}, u32[]{:S(2)}) copy-start(s32[4,64]{1,0:T(4,128)} %param.8) | copy-start | bytes 3076
  56.1 0.8 copy-start
  57.7 22.6 %collective-permute-start.1 = (bf16[2,256,128]{2,1,0:T(8,128)(2,1)}, bf16[2,256,128]{2,1,0:T(8,128)(2,1)S(1)}, u32[]{:S(2)}, u32[]{:S(2)}) collective-permute-start(bf16[2,256,128]{2,1,0:T(8,128)(2,1)} %get-tuple-element.11), channel_id=1, source_target_pairs={{0,12},{1,13},{2,14},{3,15},{16,28},{17,29},{18,30},{19,31}} | collective-permute-start | bytes 393224 | tf_op jit(solution)/shard_map/ppermute | solution.py:26
  65.7 16.5 %collective-permute-start.2 = (bf16[2,256,128]{2,1,0:T(8,128)(2,1)}, bf16[2,256,128]{2,1,0:T(8,128)(2,1)S(1)}, u32[]{:S(2)}, u32[]{:S(2)}) collective-permute-start(bf16[2,256,128]{2,1,0:T(8,128)(2,1)} %get-tuple-element.10), channel_id=1, source_target_pairs={{0,8},{4,12},{1,9},{5,13},{2,10},{6,14},{3,11},{7,15},{16,24},{20,... | collective-permute-start | bytes 393224 | tf_op jit(solution)/shard_map/ppermute | solution.py:26
  75.1 66.6 %collective-permute-start.7 = (bf16[2,128,1024]{2,1,0:T(8,128)(2,1)S(1)}, bf16[2,128,1024]{2,1,0:T(8,128)(2,1)S(1)}, u32[]{:S(2)}, u32[]{:S(2)}) collective-permute-start(bf16[2,128,1024]{2,1,0:T(8,128)(2,1)S(1)} %copy.55), channel_id=1, source_target_pairs={{0,12},{1,13},{2,14},{3,15},{16,28},{17,29},{18,30},{19,31}} | collective-permute-start | bytes 1572872 | tf_op jit(solution)/shard_map/ppermute | solution.py:26
  76.5 66.5 %collective-permute-start.8 = (bf16[2,128,1024]{2,1,0:T(8,128)(2,1)S(1)}, bf16[2,128,1024]{2,1,0:T(8,128)(2,1)S(1)}, u32[]{:S(2)}, u32[]{:S(2)}) collective-permute-start(bf16[2,128,1024]{2,1,0:T(8,128)(2,1)S(1)} %copy.55), channel_id=1, source_target_pairs={{0,8},{4,12},{1,9},{5,13},{2,10},{6,14},{3,11},{7,15},{16,24},{20,... | collective-permute-start | bytes 1572872 | tf_op jit(solution)/shard_map/ppermute | solution.py:26
  77.8 65.2 %collective-permute-start.9 = (bf16[2,128,1024]{2,1,0:T(8,128)(2,1)S(1)}, bf16[2,128,1024]{2,1,0:T(8,128)(2,1)S(1)}, u32[]{:S(2)}, u32[]{:S(2)}) collective-permute-start(bf16[2,128,1024]{2,1,0:T(8,128)(2,1)S(1)} %copy.55), channel_id=1, source_target_pairs={{0,4},{4,8},{8,12},{1,5},{5,9},{9,13},{2,6},{6,10},{10,14},{3,7},{... | collective-permute-start | bytes 1572872 | tf_op jit(solution)/shard_map/ppermute | solution.py:26
  80.3 32.5 %collective-permute-start.3 = (bf16[2,256,128]{2,1,0:T(8,128)(2,1)}, bf16[2,256,128]{2,1,0:T(8,128)(2,1)S(1)}, u32[]{:S(2)}, u32[]{:S(2)}) collective-permute-start(bf16[2,256,128]{2,1,0:T(8,128)(2,1)} %get-tuple-element.9), channel_id=1, source_target_pairs={{0,4},{4,8},{8,12},{1,5},{5,9},{9,13},{2,6},{6,10},{10,14},{3,7},{... | collective-permute-start | bytes 393224 | tf_op jit(solution)/shard_map/ppermute | solution.py:26
  82.2 33.1 %collective-permute-start.4 = (bf16[2,256,128]{2,1,0:T(8,128)(2,1)}, bf16[2,256,128]{2,1,0:T(8,128)(2,1)S(1)}, u32[]{:S(2)}, u32[]{:S(2)}) collective-permute-start(bf16[2,256,128]{2,1,0:T(8,128)(2,1)} %get-tuple-element.8), channel_id=1, source_target_pairs={{4,0},{8,4},{12,8},{5,1},{9,5},{13,9},{6,2},{10,6},{14,10},{7,3},{... | collective-permute-start | bytes 393224 | tf_op jit(solution)/shard_map/ppermute | solution.py:26
  112.8 25.3 %collective-permute-start.5 = (bf16[2,256,128]{2,1,0:T(8,128)(2,1)}, bf16[2,256,128]{2,1,0:T(8,128)(2,1)S(1)}, u32[]{:S(2)}, u32[]{:S(2)}) collective-permute-start(bf16[2,256,128]{2,1,0:T(8,128)(2,1)} %get-tuple-element.7), channel_id=1, source_target_pairs={{8,0},{12,4},{9,1},{13,5},{10,2},{14,6},{11,3},{15,7},{24,16},{28,... | collective-permute-start | bytes 393224 | tf_op jit(solution)/shard_map/ppermute | solution.py:26
  115.3 24.1 %collective-permute-start.6 = (bf16[2,256,128]{2,1,0:T(8,128)(2,1)S(1)}, bf16[2,256,128]{2,1,0:T(8,128)(2,1)S(1)}, u32[]{:S(2)}, u32[]{:S(2)}) collective-permute-start(bf16[2,256,128]{2,1,0:T(8,128)(2,1)S(1)} %get-tuple-element.6), channel_id=1, source_target_pairs={{12,0},{13,1},{14,2},{15,3},{28,16},{29,17},{30,18},{31,19}} | collective-permute-start | bytes 393224 | tf_op jit(solution)/shard_map/ppermute | solution.py:26
  138.1 16.4 %collective-permute-start.10 = (bf16[2,128,1024]{2,1,0:T(8,128)(2,1)S(1)}, bf16[2,128,1024]{2,1,0:T(8,128)(2,1)S(1)}, u32[]{:S(2)}, u32[]{:S(2)}) collective-permute-start(bf16[2,128,1024]{2,1,0:T(8,128)(2,1)S(1)} %copy.55), channel_id=1, source_target_pairs={{4,0},{8,4},{12,8},{5,1},{9,5},{13,9},{6,2},{10,6},{14,10},{7,3},{... | collective-permute-start | bytes 1572872 | tf_op jit(solution)/shard_map/ppermute | solution.py:26
  139.5 45.4 %collective-permute-start.11 = (bf16[2,128,1024]{2,1,0:T(8,128)(2,1)S(1)}, bf16[2,128,1024]{2,1,0:T(8,128)(2,1)S(1)}, u32[]{:S(2)}, u32[]{:S(2)}) collective-permute-start(bf16[2,128,1024]{2,1,0:T(8,128)(2,1)S(1)} %copy.55), channel_id=1, source_target_pairs={{8,0},{12,4},{9,1},{13,5},{10,2},{14,6},{11,3},{15,7},{24,16},{28,... | collective-permute-start | bytes 1572872 | tf_op jit(solution)/shard_map/ppermute | solution.py:26
  141.6 43.3 %collective-permute-start.12 = (bf16[2,128,1024]{2,1,0:T(8,128)(2,1)S(1)}, bf16[2,128,1024]{2,1,0:T(8,128)(2,1)S(1)}, u32[]{:S(2)}, u32[]{:S(2)}) collective-permute-start(bf16[2,128,1024]{2,1,0:T(8,128)(2,1)S(1)} %copy.55), channel_id=1, source_target_pairs={{12,0},{13,1},{14,2},{15,3},{28,16},{29,17},{30,18},{31,19}} | collective-permute-start | bytes 1572872 | tf_op jit(solution)/shard_map/ppermute | solution.py:26
Sparse Core Ops, SparseCore 0:
  53.8 13.4 reduce-scatter.1

commit v2 on v1

--- a/solution.py
+++ b/solution.py
@@ -16,7 +16,7 @@
 
 norm_ratio = 0.5
 tile_rows = 4
-chunk_rows = 256
+chunk_rows = 512
 _INTERPRET = False
 
 
@@ -128,11 +128,10 @@
     m_relative = jnp.concatenate(m_pieces, axis=1)
     m16 = lax.dynamic_slice_in_dim(m_relative, (n_tm - 1 - tm_idx) * seg16, n_tm * seg16, 1)
     m16 = jnp.pad(m16, ((0, 0), (lag_steps - 1, 0), (0, 0))).astype(jnp.float32)
-    cot16 = lax.dynamic_slice_in_dim(cotangent.reshape(seg16, band, nb, width), sub * half, half, 2)
-    onehot_mine = lax.dynamic_slice_in_dim(onehot, sub * half, half, 0).reshape(half, width, n_tm, chunk)
-    r_split = jnp.einsum(
-        "ksbi,bicr->cbsrk", cot16, onehot_mine, preferred_element_type=jnp.float32
-    ).astype(jnp.bfloat16).reshape(n_tm, half, band * chunk, seg16)
+    reord_mine = lax.dynamic_slice_in_dim(r4.reshape(nb, seg_rows, width), sub * half, half, 0)
+    r_split = jnp.transpose(
+        reord_mine.reshape(half, seg16, band, n_tm, chunk), (3, 0, 2, 4, 1)
+    ).reshape(n_tm, half, band * chunk, seg16)
     own_piece = lax.dynamic_index_in_dim(r_split, tm_idx, 0, keepdims=False)
     pieces = []
     for e in range(-(n_tm - 1), n_tm):

time: 235 us -> 216 us (0.919)
  waiting for transfers between devices: 92.4 us -> 65.9 us
  starting transfers between devices: 25.8 us -> 32.4 us
    ppermute x13, waiting for transfers between devices: 92.4 us -> 65.9 us  [passed_along(): return lax.ppermute(block, axis, route)]
    ppermute x13, starting transfers between devices: 25.8 us -> 32.4 us  [passed_along(): return lax.ppermute(block, axis, route)]
    transpose x0 -> x1, local copies, waits for them, and re-layouts: none -> 3.68 us  [local_body(): jnp.transpose(reord_mine.reshape(half, seg16, band, n_tm, chunk), (3, 0,...]
    reshape x1, local copies, waits for them, and re-layouts: 3.33 us -> 0.86 us  [local_body(): inp16 = jnp.transpose(inputs.reshape(seg16, band, nb, width), (2, 0, 1, 3))]
  transfers between devices with their start and end apart: 14 -> 14, of which waited for: 4 -> 6; matrix products, arithmetic and copies ran while one was open for 20% -> 24% of each run, Pallas kernels for 3% -> 4%
where the time goes in v2:
time: 216 us; the launch traced here: 215 us
  waiting for transfers between devices  65.9 us (31%)
  local copies, waits for them, and re-layouts  43.6 us (20%)
  starting transfers between devices  32.4 us (15%)
  blocking collectives  21.1 us (10%)
  other arithmetic  17.2 us (8%)
  Pallas kernels  16.9 us (8%)
  between operations  15.8 us (7%)
    ppermute x13, waiting for transfers between devices, passed_along(): return lax.ppermute(block, axis, route)  65.9 us
    ppermute x13, starting transfers between devices, passed_along(): return lax.ppermute(block, axis, route)  32.4 us
    psum x2, blocking collectives, local_body(): total_squares = lax.psum(lax.psum(own_squares, ('bundle', 'sub')), 'tm')  16.5 us
    slice x1, local copies, waits for them, and re-layouts, local_body(): lax.slice_in_dim(kpad, tr - 1 - u, tr - 1 - u + stripes, 1, 1)  9.53 us
    pallas_call x1, Pallas kernels, local_body(): pl.pallas_call(functools.partial(dx_kernel, lag_tiles=lag_tiles, rows=row...  8.76 us
    concatenate x1, other arithmetic, local_body(): jnp.concatenate([lax.slice_in_dim(kpad, tr - 1 - u, tr - 1 - u + stripes,...  8.24 us
    pallas_call x1, Pallas kernels, local_body(): pl.pallas_call(functools.partial(raw_kernel, lag_steps=lag_steps, rows=ro...  8.14 us
    reshape x1, local copies, waits for them, and re-layouts, local_body(): kern = impulse.reshape(nb, lag_count, width, width)  6.89 us
  transfers between devices with their start and end apart: 14, of which 6 were waited for; matrix products, arithmetic and copies ran while one was open for 24% of the time, Pallas kernels for 4%

profile of v2, /device:TPU:0, one launch (start us, length us, event | category | flops | bytes accessed | tf_op | source)
XLA Modules:
  0.0 214.9 jit_solution(11183745310879529112)
XLA Ops:
  7.2 3.3 %reshape.103 = bf16[512,4,4,64]{3,2,1,0:T(4,128)(2,1)S(1)} reshape(bf16[2048,256]{1,0:T(8,128)(2,1)} %param.5) | data formatting | bytes 2097152 | tf_op jit(solution)/shard_map/reshape | solution.py:78
  14.3 6.9 %reshape.105 = bf16[4,64,64,64]{3,2,1,0:T(8,128)(2,1)} reshape(bf16[4,64,4096]{2,1,0:T(8,128)(2,1)} %param.7) | data formatting | bytes 4194304 | tf_op jit(solution)/shard_map/reshape | solution.py:88
  21.2 9.5 %pad_slice_fusion.3 = (bf16[4,68,64,64]{3,2,1,0:T(8,128)(2,1)S(1)}, bf16[4,68,64,64]{3,2,1,0:T(8,128)(2,1)S(1)}, bf16[4,68,64,64]{3,2,1,0:T(8,128)(2,1)S(1)}, bf16[4,68,64,64]{3,2,1,0:T(8,128)(2,1)S(1)}) fusion(bf16[4,64,64,64]{3,2,1,0:T(8,128)(2,1)} %reshape.105), kind=kLoop, calls=%fused_computation.4 | loop fusion | bytes 11010048 | tf_op jit(solution)/shard_map/slice | solution.py:92
  30.8 8.2 %pad_maximum_fusion = bf16[4,68,64,256]{3,2,1,0:T(8,128)(2,1)} fusion(bf16[4,68,64,64]{3,2,1,0:T(8,128)(2,1)S(1)} %get-tuple-element.5, bf16[4,68,64,64]{3,2,1,0:T(8,128)(2,1)S(1)} %get-tuple-element.4, bf16[4,68,64,64]{3,2,1,0:T(8,128)(2,1)S(1)} %get-tuple-element.3, bf16[4,68,64,64]{3,2,1,0:T(8,128)(2,1)S(1)} %get-tuple-element.2), kind=kLoop, calls=%fused_computation | loop fusion | flops 35651584 | bytes 17825792 | tf_op jit(solution)/shard_map/concatenate | solution.py:91
  40.8 8.8 %shard_map.68 = f32[4,512,256]{2,1,0:T(8,128)} custom-call(f32[4,528,256]{2,1,0:T(8,128)} %fusion.6.r_ref, bf16[4,4352,256]{2,1,0:T(8,128)(2,1)} %bitcast.43), custom_call_target="tpu_custom_call" | custom-call | tf_op jit(solution)/shard_map/pallas_call | solution.py:95
  51.4 4.5 %reshape.109 = bf16[2,128,16,4,16]{2,1,4,3,0:T(8,128)(2,1)} reshape(bf16[2,2048,64]{1,2,0:T(8,128)(2,1)S(1)} %copy.51) | data formatting | bytes 1048576 | tf_op jit(solution)/shard_map/reshape | solution.py:133
  56.0 3.7 %copy.52 = bf16[4,2,16,16,128]{4,3,2,1,0:T(8,128)(2,1)S(1)} copy(bf16[4,2,16,16,128]{2,4,3,0,1:T(8,128)(2,1)} %bitcast.44) | data formatting | bytes 1048576 | tf_op jit(solution)/shard_map/transpose | solution.py:132
  60.6 7.6 %collective-permute-start.2 = (bf16[2,256,128]{2,1,0:T(8,128)(2,1)}, bf16[2,256,128]{2,1,0:T(8,128)(2,1)S(1)}, u32[]{:S(2)}, u32[]{:S(2)}) collective-permute-start(bf16[2,256,128]{2,1,0:T(8,128)(2,1)} %get-tuple-element.10), channel_id=1, source_target_pairs={{0,8},{4,12},{1,9},{5,13},{2,10},{6,14},{3,11},{7,15},{16,24},{20,... | collective-permute-start | bytes 393224 | tf_op jit(solution)/shard_map/ppermute | solution.py:26
  68.2 2.5 %collective-permute-start.1 = (bf16[2,256,128]{2,1,0:T(8,128)(2,1)}, bf16[2,256,128]{2,1,0:T(8,128)(2,1)S(1)}, u32[]{:S(2)}, u32[]{:S(2)}) collective-permute-start(bf16[2,256,128]{2,1,0:T(8,128)(2,1)} %get-tuple-element.11), channel_id=1, source_target_pairs={{0,12},{1,13},{2,14},{3,15},{16,28},{17,29},{18,30},{19,31}} | collective-permute-start | bytes 393224 | tf_op jit(solution)/shard_map/ppermute | solution.py:26
  72.4 2.8 %fusion.7 = bf16[2,128,16,64]{3,0,2,1:T(2,128)(2,1)S(1)} fusion(pred[128,16]{1,0:T(8,128)(4,1)S(1)} %add_compare_fusion, bf16[128,16,4,64]{3,2,1,0:T(4,128)(2,1)S(1)} %reshape.111, s32[]{:T(128)S(6)} %select_n.34), kind=kLoop, calls=%fused_computation.14 | loop fusion | flops 262144 | bytes 1050628 | tf_op jit(solution)/shard_map/jit(_where)/select_n | solution.py:118
  78.9 6.4 %collective-permute-start.7 = (bf16[2,128,1024]{2,1,0:T(8,128)(2,1)S(1)}, bf16[2,128,1024]{2,1,0:T(8,128)(2,1)S(1)}, u32[]{:S(2)}, u32[]{:S(2)}) collective-permute-start(bf16[2,128,1024]{2,1,0:T(8,128)(2,1)S(1)} %copy.54), channel_id=1, source_target_pairs={{0,12},{1,13},{2,14},{3,15},{16,28},{17,29},{18,30},{19,31}} | collective-permute-start | bytes 1572872 | tf_op jit(solution)/shard_map/ppermute | solution.py:26
  88.6 14.8 %collective-permute-done.3 = bf16[2,256,128]{2,1,0:T(8,128)(2,1)S(1)} collective-permute-done((bf16[2,256,128]{2,1,0:T(8,128)(2,1)}, bf16[2,256,128]{2,1,0:T(8,128)(2,1)S(1)}, u32[]{:S(2)}, u32[]{:S(2)}) %collective-permute-start.3) | collective-permute-done | bytes 131104 | tf_op jit(solution)/shard_map/ppermute | solution.py:26
  105.7 16.2 %collective-permute-done.4 = bf16[2,256,128]{2,1,0:T(8,128)(2,1)S(1)} collective-permute-done((bf16[2,256,128]{2,1,0:T(8,128)(2,1)}, bf16[2,256,128]{2,1,0:T(8,128)(2,1)S(1)}, u32[]{:S(2)}, u32[]{:S(2)}) %collective-permute-start.4) | collective-permute-done | bytes 131104 | tf_op jit(solution)/shard_map/ppermute | solution.py:26
  123.2 3.7 %collective-permute-start.9 = (bf16[2,128,1024]{2,1,0:T(8,128)(2,1)S(1)}, bf16[2,128,1024]{2,1,0:T(8,128)(2,1)S(1)}, u32[]{:S(2)}, u32[]{:S(2)}) collective-permute-start(bf16[2,128,1024]{2,1,0:T(8,128)(2,1)S(1)} %copy.54), channel_id=1, source_target_pairs={{0,4},{4,8},{8,12},{1,5},{5,9},{9,13},{2,6},{6,10},{10,14},{3,7},{... | collective-permute-start | bytes 1572872 | tf_op jit(solution)/shard_map/ppermute | solution.py:26
  126.9 3.6 %collective-permute-done.6 = bf16[2,256,128]{2,1,0:T(8,128)(2,1)S(1)} collective-permute-done((bf16[2,256,128]{2,1,0:T(8,128)(2,1)S(1)}, bf16[2,256,128]{2,1,0:T(8,128)(2,1)S(1)}, u32[]{:S(2)}, u32[]{:S(2)}) %collective-permute-start.6) | collective-permute-done | bytes 131104 | tf_op jit(solution)/shard_map/ppermute | solution.py:26
  134.1 3.6 %collective-permute-done.9 = bf16[2,128,1024]{2,1,0:T(8,128)(2,1)S(1)} collective-permute-done((bf16[2,128,1024]{2,1,0:T(8,128)(2,1)S(1)}, bf16[2,128,1024]{2,1,0:T(8,128)(2,1)S(1)}, u32[]{:S(2)}, u32[]{:S(2)}) %collective-permute-start.9) | collective-permute-done | bytes 524320 | tf_op jit(solution)/shard_map/ppermute | solution.py:26
  137.7 8.2 %collective-permute-done.10 = bf16[2,128,1024]{2,1,0:T(8,128)(2,1)S(1)} collective-permute-done((bf16[2,128,1024]{2,1,0:T(8,128)(2,1)S(1)}, bf16[2,128,1024]{2,1,0:T(8,128)(2,1)S(1)}, u32[]{:S(2)}, u32[]{:S(2)}) %collective-permute-start.10) | collective-permute-done | bytes 524320 | tf_op jit(solution)/shard_map/ppermute | solution.py:26
  145.9 19.6 %collective-permute-done.11 = bf16[2,128,1024]{2,1,0:T(8,128)(2,1)S(1)} collective-permute-done((bf16[2,128,1024]{2,1,0:T(8,128)(2,1)S(1)}, bf16[2,128,1024]{2,1,0:T(8,128)(2,1)S(1)}, u32[]{:S(2)}, u32[]{:S(2)}) %collective-permute-start.11) | collective-permute-done | bytes 524320 | tf_op jit(solution)/shard_map/ppermute | solution.py:26
  165.8 2.4 %pad_convert_fusion.m_ref = f32[2,520,1024]{2,1,0:T(8,128)} fusion(bf16[2,512,1024]{2,1,0:T(8,128)(2,1)S(1)} %constant_dynamic-slice_fusion), kind=kLoop, calls=%fused_computation.5 | loop fusion | flops 1064960 | bytes 6356992 | tf_op jit(solution)/shard_map/convert_element_type | solution.py:130
  168.2 8.1 %shard_map.69 = f32[2,2048,64]{2,1,0:T(8,128)} custom-call(bf16[2,256,512]{2,1,0:T(8,128)(2,1)} %constant_dynamic-slice_fusion.1.rt_ref, f32[2,520,1024]{2,1,0:T(8,128)} %pad_convert_fusion.m_ref), custom_call_target="tpu_custom_call" | custom-call | tf_op jit(solution)/shard_map/pallas_call | solution.py:146
  176.4 2.0 reshape.113
  179.2 4.6 %all_to_all.4 = f32[2,128,1024]{2,0,1:T(2,128)S(1)} all-to-all(f32[2,128,1024]{2,0,1:T(2,128)S(1)} %copy.61), channel_id=1, replica_groups=mesh['case'=2,'tm'=4,'bundle'=2,'sub'=2] {'sub'}, dimensions={1} | all-to-all | bytes 2097152 | tf_op jit(solution)/shard_map/all_to_all | solution.py:159
  185.5 7.5 %psum.14 = f32[]{:T(128)} all-reduce(f32[]{:T(128)} %multiply_reduce_fusion), channel_id=1, replica_groups=mesh['case'=2,'tm'=4,'bundle'=2,'sub'=2] {'bundle','sub'}, use_global_device_ids=true, to_apply=%region_2.3 | all-reduce | flops 1 | bytes 8 | tf_op jit(solution)/shard_map/psum | solution.py:178
  193.0 9.0 %psum.15 = f32[]{:T(128)} all-reduce(f32[]{:T(128)} %psum.14), channel_id=1, replica_groups=mesh['case'=2,'tm'=4,'bundle'=2,'sub'=2] {'tm'}, use_global_device_ids=true, to_apply=%region_3.4 | all-reduce | flops 1 | bytes 8 | tf_op jit(solution)/shard_map/psum | solution.py:178
  (62 shorter events, 31.6 us)
Async XLA Ops:
  7.2 196.9 %reduce-scatter.2.cloned.1.call-start = ((), (), s32[]{:S(2)}) async-start(), calls=%async_computation.2 | async-start | bytes 3145728 | tf_op jit(solution)/shard_map/reduce_scatter | solution.py:161
  13.0 26.0 %collective-permute-start = (bf16[4,32,256]{2,1,0:T(8,128)(2,1)S(1)}, bf16[4,32,256]{2,1,0:T(8,128)(2,1)S(1)}, u32[]{:S(2)}, u32[]{:S(2)}) collective-permute-start(bf16[4,32,256]{2,1,0:T(8,128)(2,1)S(1)} %slice.20), channel_id=1, source_target_pairs={{4,0},{8,4},{12,8},{5,1},{9,5},{13,9},{6,2},{10,6},{14,10},{7,3},{... | collective-permute-start | bytes 196616 | tf_op jit(solution)/shard_map/ppermute | solution.py:26
  56.0 15.4 %copy-start.1 = (bf16[2048,256]{1,0:T(8,128)(2,1)S(1)}, bf16[2048,256]{1,0:T(8,128)(2,1)}, u32[]{:S(2)}) copy-start(bf16[2048,256]{1,0:T(8,128)(2,1)} %param.6) | copy-start | bytes 3145732
  59.6 11.1 %copy-start = (bf16[4,2,16,16,128]{4,3,2,1,0:T(8,128)(2,1)}, bf16[4,2,16,16,128]{4,3,2,1,0:T(8,128)(2,1)S(1)}, u32[]{:S(2)}) copy-start(bf16[4,2,16,16,128]{4,3,2,1,0:T(8,128)(2,1)S(1)} %copy.52) | copy-start | bytes 1572868
  60.6 26.7 %collective-permute-start.2 = (bf16[2,256,128]{2,1,0:T(8,128)(2,1)}, bf16[2,256,128]{2,1,0:T(8,128)(2,1)S(1)}, u32[]{:S(2)}, u32[]{:S(2)}) collective-permute-start(bf16[2,256,128]{2,1,0:T(8,128)(2,1)} %get-tuple-element.10), channel_id=1, source_target_pairs={{0,8},{4,12},{1,9},{5,13},{2,10},{6,14},{3,11},{7,15},{16,24},{20,... | collective-permute-start | bytes 393224 | tf_op jit(solution)/shard_map/ppermute | solution.py:26
  68.2 17.2 %collective-permute-start.1 = (bf16[2,256,128]{2,1,0:T(8,128)(2,1)}, bf16[2,256,128]{2,1,0:T(8,128)(2,1)S(1)}, u32[]{:S(2)}, u32[]{:S(2)}) collective-permute-start(bf16[2,256,128]{2,1,0:T(8,128)(2,1)} %get-tuple-element.11), channel_id=1, source_target_pairs={{0,12},{1,13},{2,14},{3,15},{16,28},{17,29},{18,30},{19,31}} | collective-permute-start | bytes 393224 | tf_op jit(solution)/shard_map/ppermute | solution.py:26
  76.3 89.2 %collective-permute-start.12 = (bf16[2,128,1024]{2,1,0:T(8,128)(2,1)S(1)}, bf16[2,128,1024]{2,1,0:T(8,128)(2,1)S(1)}, u32[]{:S(2)}, u32[]{:S(2)}) collective-permute-start(bf16[2,128,1024]{2,1,0:T(8,128)(2,1)S(1)} %copy.54), channel_id=1, source_target_pairs={{12,0},{13,1},{14,2},{15,3},{28,16},{29,17},{30,18},{31,19}} | collective-permute-start | bytes 1572872 | tf_op jit(solution)/shard_map/ppermute | solution.py:26
  77.6 56.4 %collective-permute-start.8 = (bf16[2,128,1024]{2,1,0:T(8,128)(2,1)S(1)}, bf16[2,128,1024]{2,1,0:T(8,128)(2,1)S(1)}, u32[]{:S(2)}, u32[]{:S(2)}) collective-permute-start(bf16[2,128,1024]{2,1,0:T(8,128)(2,1)S(1)} %copy.54), channel_id=1, source_target_pairs={{0,8},{4,12},{1,9},{5,13},{2,10},{6,14},{3,11},{7,15},{16,24},{20,... | collective-permute-start | bytes 1572872 | tf_op jit(solution)/shard_map/ppermute | solution.py:26
  78.9 53.7 %collective-permute-start.7 = (bf16[2,128,1024]{2,1,0:T(8,128)(2,1)S(1)}, bf16[2,128,1024]{2,1,0:T(8,128)(2,1)S(1)}, u32[]{:S(2)}, u32[]{:S(2)}) collective-permute-start(bf16[2,128,1024]{2,1,0:T(8,128)(2,1)S(1)} %copy.54), channel_id=1, source_target_pairs={{0,12},{1,13},{2,14},{3,15},{16,28},{17,29},{18,30},{19,31}} | collective-permute-start | bytes 1572872 | tf_op jit(solution)/shard_map/ppermute | solution.py:26
  85.3 18.1 %collective-permute-start.3 = (bf16[2,256,128]{2,1,0:T(8,128)(2,1)}, bf16[2,256,128]{2,1,0:T(8,128)(2,1)S(1)}, u32[]{:S(2)}, u32[]{:S(2)}) collective-permute-start(bf16[2,256,128]{2,1,0:T(8,128)(2,1)} %get-tuple-element.9), channel_id=1, source_target_pairs={{0,4},{4,8},{8,12},{1,5},{5,9},{9,13},{2,6},{6,10},{10,14},{3,7},{... | collective-permute-start | bytes 393224 | tf_op jit(solution)/shard_map/ppermute | solution.py:26
  87.3 35.9 %collective-permute-start.5 = (bf16[2,256,128]{2,1,0:T(8,128)(2,1)}, bf16[2,256,128]{2,1,0:T(8,128)(2,1)S(1)}, u32[]{:S(2)}, u32[]{:S(2)}) collective-permute-start(bf16[2,256,128]{2,1,0:T(8,128)(2,1)} %get-tuple-element.7), channel_id=1, source_target_pairs={{8,0},{12,4},{9,1},{13,5},{10,2},{14,6},{11,3},{15,7},{24,16},{28,... | collective-permute-start | bytes 393224 | tf_op jit(solution)/shard_map/ppermute | solution.py:26
  103.4 18.4 %collective-permute-start.4 = (bf16[2,256,128]{2,1,0:T(8,128)(2,1)}, bf16[2,256,128]{2,1,0:T(8,128)(2,1)S(1)}, u32[]{:S(2)}, u32[]{:S(2)}) collective-permute-start(bf16[2,256,128]{2,1,0:T(8,128)(2,1)} %get-tuple-element.8), channel_id=1, source_target_pairs={{4,0},{8,4},{12,8},{5,1},{9,5},{13,9},{6,2},{10,6},{14,10},{7,3},{... | collective-permute-start | bytes 393224 | tf_op jit(solution)/shard_map/ppermute | solution.py:26
  121.9 8.6 %collective-permute-start.6 = (bf16[2,256,128]{2,1,0:T(8,128)(2,1)S(1)}, bf16[2,256,128]{2,1,0:T(8,128)(2,1)S(1)}, u32[]{:S(2)}, u32[]{:S(2)}) collective-permute-start(bf16[2,256,128]{2,1,0:T(8,128)(2,1)S(1)} %get-tuple-element.6), channel_id=1, source_target_pairs={{12,0},{13,1},{14,2},{15,3},{28,16},{29,17},{30,18},{31,19}} | collective-permute-start | bytes 393224 | tf_op jit(solution)/shard_map/ppermute | solution.py:26
  123.2 14.4 %collective-permute-start.9 = (bf16[2,128,1024]{2,1,0:T(8,128)(2,1)S(1)}, bf16[2,128,1024]{2,1,0:T(8,128)(2,1)S(1)}, u32[]{:S(2)}, u32[]{:S(2)}) collective-permute-start(bf16[2,128,1024]{2,1,0:T(8,128)(2,1)S(1)} %copy.54), channel_id=1, source_target_pairs={{0,4},{4,8},{8,12},{1,5},{5,9},{9,13},{2,6},{6,10},{10,14},{3,7},{... | collective-permute-start | bytes 1572872 | tf_op jit(solution)/shard_map/ppermute | solution.py:26
  130.5 15.4 %collective-permute-start.10 = (bf16[2,128,1024]{2,1,0:T(8,128)(2,1)S(1)}, bf16[2,128,1024]{2,1,0:T(8,128)(2,1)S(1)}, u32[]{:S(2)}, u32[]{:S(2)}) collective-permute-start(bf16[2,128,1024]{2,1,0:T(8,128)(2,1)S(1)} %copy.54), channel_id=1, source_target_pairs={{4,0},{8,4},{12,8},{5,1},{9,5},{13,9},{6,2},{10,6},{14,10},{7,3},{... | collective-permute-start | bytes 1572872 | tf_op jit(solution)/shard_map/ppermute | solution.py:26
  132.7 32.8 %collective-permute-start.11 = (bf16[2,128,1024]{2,1,0:T(8,128)(2,1)S(1)}, bf16[2,128,1024]{2,1,0:T(8,128)(2,1)S(1)}, u32[]{:S(2)}, u32[]{:S(2)}) collective-permute-start(bf16[2,128,1024]{2,1,0:T(8,128)(2,1)S(1)} %copy.54), channel_id=1, source_target_pairs={{8,0},{12,4},{9,1},{13,5},{10,2},{14,6},{11,3},{15,7},{24,16},{28,... | collective-permute-start | bytes 1572872 | tf_op jit(solution)/shard_map/ppermute | solution.py:26
Sparse Core Ops, SparseCore 0:
  49.7 13.4 reduce-scatter.1

commit v3 on v2

--- a/solution.py
+++ b/solution.py
@@ -32,13 +32,17 @@
 
 def dx_kernel(r_ref, t_ref, o_ref, *, lag_tiles, rows):
     width = o_ref.shape[2]
-    width_t = t_ref.shape[2]
+    cb = t_ref.shape[2]
     for c in range(rows // chunk_rows):
         base = c * chunk_rows
         acc = jnp.zeros((chunk_rows, width), jnp.float32)
         for q in range(lag_tiles):
             x = r_ref[0, base + q : base + q + chunk_rows, :].astype(jnp.bfloat16)
-            acc = acc + jnp.dot(x, t_ref[0, q * width_t : (q + 1) * width_t, :], preferred_element_type=jnp.float32)
+            blk = jnp.concatenate(
+                [t_ref[0, (tile_rows * q + tile_rows - 1 - u) * cb : (tile_rows * q + 2 * tile_rows - 1 - u) * cb, :] for u in range(tile_rows)],
+                axis=1,
+            )
+            acc = acc + jnp.dot(x, blk, preferred_element_type=jnp.float32)
         o_ref[0, base : base + chunk_rows, :] = acc
 
 
@@ -83,21 +87,18 @@
 
     seg_start = lax.axis_index("tm") * seg_rows
     ahead = passed_along(r4[:, :halo], "tm", -1)
-    r4ext = jnp.concatenate([r4, ahead], axis=1).astype(jnp.float32)
+    r4ext = jnp.concatenate([r4, ahead], axis=1)
     r4w = lax.dynamic_slice_in_dim(r4ext, sub * shift, rows4 + shift, 1)
     kern = impulse.reshape(nb, lag_count, width, width)
     kpad = jnp.pad(kern, ((0, 0), (tr - 1, tr), (0, 0), (0, 0)))
-    stripes = tr * lag_tiles
-    toeplitz = jnp.concatenate(
-        [lax.slice_in_dim(kpad, tr - 1 - u, tr - 1 - u + stripes, 1, 1) for u in range(tr)], axis=3
-    ).reshape(nb, stripes * width, wide)
+    toeplitz = kpad.reshape(nb, (lag_count + 2 * tr - 1) * width, width)
 
     partial_dx = pl.pallas_call(
         functools.partial(dx_kernel, lag_tiles=lag_tiles, rows=rows4),
         grid=(nb,),
         in_specs=[
             pl.BlockSpec((1, rows4 + shift, wide), lambda b: (b, 0, 0)),
-            pl.BlockSpec((1, tr * lag_tiles * width, wide), lambda b: (b, 0, 0)),
+            pl.BlockSpec((1, (lag_count + 2 * tr - 1) * width, width), lambda b: (b, 0, 0)),
         ],
         out_specs=pl.BlockSpec((1, rows4, wide), lambda b: (b, 0, 0)),
         out_shape=jax.ShapeDtypeStruct((nb, rows4, wide), jnp.float32),

time: 216 us -> 223 us (1.032)
  waiting for transfers between devices: 65.9 us -> 92.4 us
  other arithmetic: 17.2 us -> 8.64 us
  starting transfers between devices: 32.4 us -> 26.2 us
  local copies, waits for them, and re-layouts: 43.6 us -> 39.9 us
    ppermute x13, waiting for transfers between devices: 65.9 us -> 92.3 us  [passed_along(): return lax.ppermute(block, axis, route)]
    slice x1 -> x0, local copies, waits for them, and re-layouts: 9.53 us -> none  [local_body(): lax.slice_in_dim(kpad, tr - 1 - u, tr - 1 - u + stripes, 1, 1)]
    concatenate x1, other arithmetic: 8.24 us -> 1.44 us  [local_body(): r4ext = jnp.concatenate([r4, ahead], axis=1)]
    ppermute x13, starting transfers between devices: 32.4 us -> 26.1 us  [passed_along(): return lax.ppermute(block, axis, route)]
    pad x0 -> x1, local copies, waits for them, and re-layouts: none -> 5.71 us  [local_body(): kpad = jnp.pad(kern, ((0, 0), (tr - 1, tr), (0, 0), (0, 0)))]
  transfers between devices with their start and end apart: 14 -> 14, of which waited for: 6 -> 4; matrix products, arithmetic and copies ran while one was open for 24% -> 18% of each run, Pallas kernels for 4% -> 4%
where the time goes in v3:
time: 223 us; the launch traced here: 222 us
  waiting for transfers between devices  92.4 us (41%)
  local copies, waits for them, and re-layouts  39.9 us (18%)
  starting transfers between devices  26.2 us (12%)
  blocking collectives  21.1 us (9%)
  Pallas kernels  16.2 us (7%)
  between operations  15.8 us (7%)
  other arithmetic  8.64 us (4%)
    ppermute x13, waiting for transfers between devices, passed_along(): return lax.ppermute(block, axis, route)  92.3 us
    ppermute x13, starting transfers between devices, passed_along(): return lax.ppermute(block, axis, route)  26.1 us
    psum x2, blocking collectives, local_body(): total_squares = lax.psum(lax.psum(own_squares, ('bundle', 'sub')), 'tm')  16.5 us
    pallas_call x1, Pallas kernels, local_body(): pl.pallas_call(functools.partial(raw_kernel, lag_steps=lag_steps, rows=ro...  8.22 us
    pallas_call x1, Pallas kernels, local_body(): pl.pallas_call(functools.partial(dx_kernel, lag_tiles=lag_tiles, rows=row...  7.97 us
    reshape x1, local copies, waits for them, and re-layouts, local_body(): kern = impulse.reshape(nb, lag_count, width, width)  6.98 us
    pad x1, local copies, waits for them, and re-layouts, local_body(): kpad = jnp.pad(kern, ((0, 0), (tr - 1, tr), (0, 0), (0, 0)))  5.71 us
    all_to_all x1, blocking collectives, local_body(): own_raw = lax.all_to_all(raw_half, 'sub', 1, 0, tiled=True)  4.58 us
  transfers between devices with their start and end apart: 14, of which 4 were waited for; matrix products, arithmetic and copies ran while one was open for 18% of the time, Pallas kernels for 4%

profile of v3, /device:TPU:0, one launch (start us, length us, event | category | flops | bytes accessed | tf_op | source)
XLA Modules:
  0.0 222.1 jit_solution(2465104402663419348)
XLA Ops:
  7.2 3.3 %reshape.103 = bf16[512,4,4,64]{3,2,1,0:T(4,128)(2,1)S(1)} reshape(bf16[2048,256]{1,0:T(8,128)(2,1)} %param.5) | data formatting | bytes 2097152 | tf_op jit(solution)/shard_map/reshape | solution.py:82
  10.5 2.0 fusion.2
  14.3 7.0 %reshape.105 = bf16[4,64,64,64]{3,2,1,0:T(8,128)(2,1)} reshape(bf16[4,64,4096]{2,1,0:T(8,128)(2,1)} %param.7) | data formatting | bytes 4194304 | tf_op jit(solution)/shard_map/reshape | solution.py:92
  21.3 5.7 %pad.8 = bf16[4,71,64,64]{3,2,1,0:T(8,128)(2,1)} pad(bf16[4,64,64,64]{3,2,1,0:T(8,128)(2,1)} %reshape.105, bf16[]{:T(256)} %constant.65.clone.1), padding=0_0x3_4x0_0x0_0 | pad | bytes 4423682 | tf_op jit(solution)/shard_map/jit(_pad)/pad | solution.py:93
  28.5 8.0 %shard_map.68 = f32[4,512,256]{2,1,0:T(8,128)} custom-call(bf16[4,528,256]{2,1,0:T(8,128)(2,1)} %fusion.5.r_ref, bf16[4,4544,64]{2,1,0:T(8,128)(2,1)} %bitcast.43), custom_call_target="tpu_custom_call" | custom-call | tf_op jit(solution)/shard_map/pallas_call | solution.py:96
  38.3 4.6 %reshape.109 = bf16[2,128,16,4,16]{2,1,4,3,0:T(8,128)(2,1)} reshape(bf16[2,2048,64]{1,2,0:T(8,128)(2,1)S(1)} %copy.51) | data formatting | bytes 1048576 | tf_op jit(solution)/shard_map/reshape | solution.py:134
  42.9 3.7 %copy.52 = bf16[4,2,16,16,128]{4,3,2,1,0:T(8,128)(2,1)S(1)} copy(bf16[4,2,16,16,128]{2,4,3,0,1:T(8,128)(2,1)} %bitcast.44) | data formatting | bytes 1048576 | tf_op jit(solution)/shard_map/transpose | solution.py:133
  47.5 8.6 %collective-permute-start.1 = (bf16[2,256,128]{2,1,0:T(8,128)(2,1)}, bf16[2,256,128]{2,1,0:T(8,128)(2,1)S(1)}, u32[]{:S(2)}, u32[]{:S(2)}) collective-permute-start(bf16[2,256,128]{2,1,0:T(8,128)(2,1)} %get-tuple-element.7), channel_id=1, source_target_pairs={{0,12},{1,13},{2,14},{3,15},{16,28},{17,29},{18,30},{19,31}} | collective-permute-start | bytes 393224 | tf_op jit(solution)/shard_map/ppermute | solution.py:26
  59.1 2.8 %fusion.6 = bf16[2,128,16,64]{3,0,2,1:T(2,128)(2,1)S(1)} fusion(pred[128,16]{1,0:T(8,128)(4,1)S(1)} %add_compare_fusion, bf16[128,16,4,64]{3,2,1,0:T(4,128)(2,1)S(1)} %reshape.111, s32[]{:T(128)S(6)} %select_n.34), kind=kLoop, calls=%fused_computation.8 | loop fusion | flops 262144 | bytes 1050628 | tf_op jit(solution)/shard_map/jit(_where)/select_n | solution.py:119
  65.7 2.5 %collective-permute-start.9 = (bf16[2,128,1024]{2,1,0:T(8,128)(2,1)S(1)}, bf16[2,128,1024]{2,1,0:T(8,128)(2,1)S(1)}, u32[]{:S(2)}, u32[]{:S(2)}) collective-permute-start(bf16[2,128,1024]{2,1,0:T(8,128)(2,1)S(1)} %copy.54), channel_id=1, source_target_pairs={{0,4},{4,8},{8,12},{1,5},{5,9},{9,13},{2,6},{6,10},{10,14},{3,7},{... | collective-permute-start | bytes 1572872 | tf_op jit(solution)/shard_map/ppermute | solution.py:26
  68.2 1.9 collective-permute-start.3
  71.5 28.7 %collective-permute-done.3 = bf16[2,256,128]{2,1,0:T(8,128)(2,1)S(1)} collective-permute-done((bf16[2,256,128]{2,1,0:T(8,128)(2,1)}, bf16[2,256,128]{2,1,0:T(8,128)(2,1)S(1)}, u32[]{:S(2)}, u32[]{:S(2)}) %collective-permute-start.3) | collective-permute-done | bytes 131104 | tf_op jit(solution)/shard_map/ppermute | solution.py:26
  103.8 22.1 %collective-permute-done.5 = bf16[2,256,128]{2,1,0:T(8,128)(2,1)S(1)} collective-permute-done((bf16[2,256,128]{2,1,0:T(8,128)(2,1)}, bf16[2,256,128]{2,1,0:T(8,128)(2,1)S(1)}, u32[]{:S(2)}, u32[]{:S(2)}) %collective-permute-start.5) | collective-permute-done | bytes 131104 | tf_op jit(solution)/shard_map/ppermute | solution.py:26
  129.4 1.5 collective-permute-start.12
  131.1 11.2 %collective-permute-done.10 = bf16[2,128,1024]{2,1,0:T(8,128)(2,1)S(1)} collective-permute-done((bf16[2,128,1024]{2,1,0:T(8,128)(2,1)S(1)}, bf16[2,128,1024]{2,1,0:T(8,128)(2,1)S(1)}, u32[]{:S(2)}, u32[]{:S(2)}) %collective-permute-start.10) | collective-permute-done | bytes 524320 | tf_op jit(solution)/shard_map/ppermute | solution.py:26
  142.4 30.3 %collective-permute-done.11 = bf16[2,128,1024]{2,1,0:T(8,128)(2,1)S(1)} collective-permute-done((bf16[2,128,1024]{2,1,0:T(8,128)(2,1)S(1)}, bf16[2,128,1024]{2,1,0:T(8,128)(2,1)S(1)}, u32[]{:S(2)}, u32[]{:S(2)}) %collective-permute-start.11) | collective-permute-done | bytes 524320 | tf_op jit(solution)/shard_map/ppermute | solution.py:26
  172.9 2.4 %pad_convert_fusion.m_ref = f32[2,520,1024]{2,1,0:T(8,128)} fusion(bf16[2,512,1024]{2,1,0:T(8,128)(2,1)S(1)} %constant_dynamic-slice_fusion), kind=kLoop, calls=%fused_computation | loop fusion | flops 1064960 | bytes 6356992 | tf_op jit(solution)/shard_map/convert_element_type | solution.py:131
  175.4 8.2 %shard_map.69 = f32[2,2048,64]{2,1,0:T(8,128)} custom-call(bf16[2,256,512]{2,1,0:T(8,128)(2,1)} %constant_dynamic-slice_fusion.1.rt_ref, f32[2,520,1024]{2,1,0:T(8,128)} %pad_convert_fusion.m_ref), custom_call_target="tpu_custom_call" | custom-call | tf_op jit(solution)/shard_map/pallas_call | solution.py:147
  183.6 2.0 reshape.113
  186.4 4.6 %all_to_all.4 = f32[2,128,1024]{2,0,1:T(2,128)S(1)} all-to-all(f32[2,128,1024]{2,0,1:T(2,128)S(1)} %copy.61), channel_id=1, replica_groups=mesh['case'=2,'tm'=4,'bundle'=2,'sub'=2] {'sub'}, dimensions={1} | all-to-all | bytes 2097152 | tf_op jit(solution)/shard_map/all_to_all | solution.py:160
  191.0 1.7 multiply_reduce_fusion
  192.7 7.5 %psum.14 = f32[]{:T(128)} all-reduce(f32[]{:T(128)} %multiply_reduce_fusion), channel_id=1, replica_groups=mesh['case'=2,'tm'=4,'bundle'=2,'sub'=2] {'bundle','sub'}, use_global_device_ids=true, to_apply=%region_2.3 | all-reduce | flops 1 | bytes 8 | tf_op jit(solution)/shard_map/psum | solution.py:179
  200.2 9.0 %psum.15 = f32[]{:T(128)} all-reduce(f32[]{:T(128)} %psum.14), channel_id=1, replica_groups=mesh['case'=2,'tm'=4,'bundle'=2,'sub'=2] {'tm'}, use_global_device_ids=true, to_apply=%region_3.4 | all-reduce | flops 1 | bytes 8 | tf_op jit(solution)/shard_map/psum | solution.py:179
  213.8 1.5 reshape.108
  (61 shorter events, 25.6 us)
Async XLA Ops:
  7.2 204.1 %reduce-scatter.2.cloned.1.call-start = ((), (), s32[]{:S(2)}) async-start(), calls=%async_computation.2 | async-start | bytes 3145728 | tf_op jit(solution)/shard_map/reduce_scatter | solution.py:162
  13.0 14.0 %collective-permute-start = (bf16[4,32,256]{2,1,0:T(8,128)(2,1)S(1)}, bf16[4,32,256]{2,1,0:T(8,128)(2,1)S(1)}, u32[]{:S(2)}, u32[]{:S(2)}) collective-permute-start(bf16[4,32,256]{2,1,0:T(8,128)(2,1)S(1)} %slice.4), channel_id=1, source_target_pairs={{4,0},{8,4},{12,8},{5,1},{9,5},{13,9},{6,2},{10,6},{14,10},{7,3},{... | collective-permute-start | bytes 196616 | tf_op jit(solution)/shard_map/ppermute | solution.py:26
  42.9 15.3 %copy-start.1 = (bf16[2048,256]{1,0:T(8,128)(2,1)S(1)}, bf16[2048,256]{1,0:T(8,128)(2,1)}, u32[]{:S(2)}) copy-start(bf16[2048,256]{1,0:T(8,128)(2,1)} %param.6) | copy-start | bytes 3145732
  46.5 11.6 %copy-start = (bf16[4,2,16,16,128]{4,3,2,1,0:T(8,128)(2,1)}, bf16[4,2,16,16,128]{4,3,2,1,0:T(8,128)(2,1)S(1)}, u32[]{:S(2)}) copy-start(bf16[4,2,16,16,128]{4,3,2,1,0:T(8,128)(2,1)S(1)} %copy.52) | copy-start | bytes 1572868
  47.5 20.7 %collective-permute-start.1 = (bf16[2,256,128]{2,1,0:T(8,128)(2,1)}, bf16[2,256,128]{2,1,0:T(8,128)(2,1)S(1)}, u32[]{:S(2)}, u32[]{:S(2)}) collective-permute-start(bf16[2,256,128]{2,1,0:T(8,128)(2,1)} %get-tuple-element.7), channel_id=1, source_target_pairs={{0,12},{1,13},{2,14},{3,15},{16,28},{17,29},{18,30},{19,31}} | collective-permute-start | bytes 393224 | tf_op jit(solution)/shard_map/ppermute | solution.py:26
  56.2 14.0 %collective-permute-start.2 = (bf16[2,256,128]{2,1,0:T(8,128)(2,1)}, bf16[2,256,128]{2,1,0:T(8,128)(2,1)S(1)}, u32[]{:S(2)}, u32[]{:S(2)}) collective-permute-start(bf16[2,256,128]{2,1,0:T(8,128)(2,1)} %get-tuple-element.6), channel_id=1, source_target_pairs={{0,8},{4,12},{1,9},{5,13},{2,10},{6,14},{3,11},{7,15},{16,24},{20,... | collective-permute-start | bytes 393224 | tf_op jit(solution)/shard_map/ppermute | solution.py:26
  63.0 66.4 %collective-permute-start.7 = (bf16[2,128,1024]{2,1,0:T(8,128)(2,1)S(1)}, bf16[2,128,1024]{2,1,0:T(8,128)(2,1)S(1)}, u32[]{:S(2)}, u32[]{:S(2)}) collective-permute-start(bf16[2,128,1024]{2,1,0:T(8,128)(2,1)S(1)} %copy.54), channel_id=1, source_target_pairs={{0,12},{1,13},{2,14},{3,15},{16,28},{17,29},{18,30},{19,31}} | collective-permute-start | bytes 1572872 | tf_op jit(solution)/shard_map/ppermute | solution.py:26
  64.4 66.6 %collective-permute-start.8 = (bf16[2,128,1024]{2,1,0:T(8,128)(2,1)S(1)}, bf16[2,128,1024]{2,1,0:T(8,128)(2,1)S(1)}, u32[]{:S(2)}, u32[]{:S(2)}) collective-permute-start(bf16[2,128,1024]{2,1,0:T(8,128)(2,1)S(1)} %copy.54), channel_id=1, source_target_pairs={{0,8},{4,12},{1,9},{5,13},{2,10},{6,14},{3,11},{7,15},{16,24},{20,... | collective-permute-start | bytes 1572872 | tf_op jit(solution)/shard_map/ppermute | solution.py:26
  65.7 65.3 %collective-permute-start.9 = (bf16[2,128,1024]{2,1,0:T(8,128)(2,1)S(1)}, bf16[2,128,1024]{2,1,0:T(8,128)(2,1)S(1)}, u32[]{:S(2)}, u32[]{:S(2)}) collective-permute-start(bf16[2,128,1024]{2,1,0:T(8,128)(2,1)S(1)} %copy.54), channel_id=1, source_target_pairs={{0,4},{4,8},{8,12},{1,5},{5,9},{9,13},{2,6},{6,10},{10,14},{3,7},{... | collective-permute-start | bytes 1572872 | tf_op jit(solution)/shard_map/ppermute | solution.py:26
  68.2 32.0 %collective-permute-start.3 = (bf16[2,256,128]{2,1,0:T(8,128)(2,1)}, bf16[2,256,128]{2,1,0:T(8,128)(2,1)S(1)}, u32[]{:S(2)}, u32[]{:S(2)}) collective-permute-start(bf16[2,256,128]{2,1,0:T(8,128)(2,1)} %get-tuple-element.5), channel_id=1, source_target_pairs={{0,4},{4,8},{8,12},{1,5},{5,9},{9,13},{2,6},{6,10},{10,14},{3,7},{... | collective-permute-start | bytes 393224 | tf_op jit(solution)/shard_map/ppermute | solution.py:26
  70.1 32.3 %collective-permute-start.4 = (bf16[2,256,128]{2,1,0:T(8,128)(2,1)}, bf16[2,256,128]{2,1,0:T(8,128)(2,1)S(1)}, u32[]{:S(2)}, u32[]{:S(2)}) collective-permute-start(bf16[2,256,128]{2,1,0:T(8,128)(2,1)} %get-tuple-element.4), channel_id=1, source_target_pairs={{4,0},{8,4},{12,8},{5,1},{9,5},{13,9},{6,2},{10,6},{14,10},{7,3},{... | collective-permute-start | bytes 393224 | tf_op jit(solution)/shard_map/ppermute | solution.py:26
  100.2 25.7 %collective-permute-start.5 = (bf16[2,256,128]{2,1,0:T(8,128)(2,1)}, bf16[2,256,128]{2,1,0:T(8,128)(2,1)S(1)}, u32[]{:S(2)}, u32[]{:S(2)}) collective-permute-start(bf16[2,256,128]{2,1,0:T(8,128)(2,1)} %get-tuple-element.3), channel_id=1, source_target_pairs={{8,0},{12,4},{9,1},{13,5},{10,2},{14,6},{11,3},{15,7},{24,16},{28,... | collective-permute-start | bytes 393224 | tf_op jit(solution)/shard_map/ppermute | solution.py:26
  102.5 24.8 %collective-permute-start.6 = (bf16[2,256,128]{2,1,0:T(8,128)(2,1)S(1)}, bf16[2,256,128]{2,1,0:T(8,128)(2,1)S(1)}, u32[]{:S(2)}, u32[]{:S(2)}) collective-permute-start(bf16[2,256,128]{2,1,0:T(8,128)(2,1)S(1)} %get-tuple-element.2), channel_id=1, source_target_pairs={{12,0},{13,1},{14,2},{15,3},{28,16},{29,17},{30,18},{31,19}} | collective-permute-start | bytes 393224 | tf_op jit(solution)/shard_map/ppermute | solution.py:26
  125.9 16.4 %collective-permute-start.10 = (bf16[2,128,1024]{2,1,0:T(8,128)(2,1)S(1)}, bf16[2,128,1024]{2,1,0:T(8,128)(2,1)S(1)}, u32[]{:S(2)}, u32[]{:S(2)}) collective-permute-start(bf16[2,128,1024]{2,1,0:T(8,128)(2,1)S(1)} %copy.54), channel_id=1, source_target_pairs={{4,0},{8,4},{12,8},{5,1},{9,5},{13,9},{6,2},{10,6},{14,10},{7,3},{... | collective-permute-start | bytes 1572872 | tf_op jit(solution)/shard_map/ppermute | solution.py:26
  127.2 45.4 %collective-permute-start.11 = (bf16[2,128,1024]{2,1,0:T(8,128)(2,1)S(1)}, bf16[2,128,1024]{2,1,0:T(8,128)(2,1)S(1)}, u32[]{:S(2)}, u32[]{:S(2)}) collective-permute-start(bf16[2,128,1024]{2,1,0:T(8,128)(2,1)S(1)} %copy.54), channel_id=1, source_target_pairs={{8,0},{12,4},{9,1},{13,5},{10,2},{14,6},{11,3},{15,7},{24,16},{28,... | collective-permute-start | bytes 1572872 | tf_op jit(solution)/shard_map/ppermute | solution.py:26
  129.4 43.3 %collective-permute-start.12 = (bf16[2,128,1024]{2,1,0:T(8,128)(2,1)S(1)}, bf16[2,128,1024]{2,1,0:T(8,128)(2,1)S(1)}, u32[]{:S(2)}, u32[]{:S(2)}) collective-permute-start(bf16[2,128,1024]{2,1,0:T(8,128)(2,1)S(1)} %copy.54), channel_id=1, source_target_pairs={{12,0},{13,1},{14,2},{15,3},{28,16},{29,17},{30,18},{31,19}} | collective-permute-start | bytes 1572872 | tf_op jit(solution)/shard_map/ppermute | solution.py:26
Sparse Core Ops, SparseCore 0:
  36.6 13.4 reduce-scatter.1
